TPU v7x, 128 devices: a whole 4x4x4 slice. The times are simulated.
128 devices in a mesh: gx: 4 (over x), gy: 16 (over z, y), wa: 2 (over core).
Axes of the slice: x: 4, y: 4, z: 4, core: 2. Of those that a mesh axis runs over, the one named last changes fastest.
Arguments:
- pressure: float32 [24, 256, 512], P(None, ('gy', 'wa'), 'gx'), may hold values from -6 to 6
- saturation: float32 [24, 256, 512], P(None, ('gy', 'wa'), 'gx'), may hold values from 0.1 to 0.9
- sat_old: float32 [24, 256, 512], P(None, ('gy', 'wa'), 'gx'), may hold values from 0.1 to 0.9
- pore: float32 [24, 256, 512], P(None, ('gy', 'wa'), 'gx'), may hold values from 0.5 to 2
- trans_x: float32 [24, 256, 512], P(None, ('gy', 'wa'), 'gx'), may hold values from 0.3 to 3
- trans_y: float32 [24, 256, 512], P(None, ('gy', 'wa'), 'gx'), may hold values from 0.3 to 3
- trans_z: float32 [24, 256, 512], P(None, ('gy', 'wa'), 'gx'), may hold values from 0.3 to 3
- upwind_x: int32 [24, 256, 512], P(None, ('gy', 'wa'), 'gx'), may hold values 0 or 1
- upwind_y: int32 [24, 256, 512], P(None, ('gy', 'wa'), 'gx'), may hold values 0 or 1
- upwind_z: int32 [24, 256, 512], P(None, ('gy', 'wa'), 'gx'), may hold values 0 or 1
- directions: float32 [4, 2, 24, 256, 512], P(None, None, None, ('gy', 'wa'), 'gx'), may hold values from -6 to 6
- adjoint_weights: float32 [4, 2, 24, 256, 512], P(None, None, None, ('gy', 'wa'), 'gx'), may hold values from -6 to 6
- perf_well: int32 [4096], P(('gx', 'gy', 'wa')), may hold values from 0 to 2047, as said below
- perf_col: int32 [4096], P(('gx', 'gy', 'wa')), may hold values from 0 to 1023
- perf_top: int32 [4096], P(('gx', 'gy', 'wa')), may hold values from 0 to 11
- perf_span: int32 [4096], P(('gx', 'gy', 'wa')), may hold values from 1 to 12
- perf_index: float32 [4096], P(('gx', 'gy', 'wa')), may hold values from 0.5 to 2
- bhp: float32 [2048], replicated, may hold values from -6 to 6
- target: float32 [2048], replicated, may hold values from -4 to 4
Outputs:
- reduced_residual: float32 [2, 24, 256, 512], P(None, None, ('gy', 'wa'), 'gx')
- forward_products: float32 [4, 2, 24, 256, 512], P(None, None, None, ('gy', 'wa'), 'gx')
- adjoint_products: float32 [4, 2, 24, 256, 512], P(None, None, None, ('gy', 'wa'), 'gx')
Inputs may be any that keep to these rules, and one draw needn't show every extreme that they name: `perf_well`: every well is named by at least one perforation row; well w is owned by device w // 16 of the axes gx+gy+wa.
All inputs are finite; a program needn't handle non-finite values. No bound on the sum of `upwind_x` or of `upwind_y` or of `upwind_z` on one device may be relied on, other than what follows from the above.
Results may differ from a plain program's by a relative error of at most 0.0002.
Values sent between devices are 32-bit elements; how exact they have to be, the bound alone decides.
No kernel may reach another device: no remote copies, remote signals or barrier semaphores. Data moves between devices by JAX's collectives and lax.ppermute only.
A program may use at most 64 MiB of HBM per device.

v0:
```python
import jax
import jax.numpy as jnp
from jax import lax
from jax.experimental import pallas as pl
from jax.experimental.pallas import tpu as pltpu
from jax.sharding import Mesh
from jax.sharding import PartitionSpec as P


GY_WA = ("gy_0", "gy_1", "wa")
GX_GY_WA = ("gx", "gy_0", "gy_1", "wa")


water_visc = 0.5
oil_visc = 2.0
water_head = 0.3
oil_head = 0.2


def gather_everywhere(block):
    peers = lax.axis_size(GX_GY_WA)
    flat = jnp.broadcast_to(block.reshape(1, -1), (peers, block.size))
    return lax.all_to_all(flat, GX_GY_WA, 0, 0, tiled=True).reshape((peers,) + block.shape)


def shift_along(block, axis, down):
    size = lax.axis_size(axis)
    pairs = [(i, i + 1) for i in range(size - 1)]
    if not down:
        pairs = [(b, a) for a, b in pairs]
    return lax.ppermute(block, axis, pairs)


def mobility(sat):
    return jnp.stack([sat * sat / water_visc, (1.0 - sat) * (1.0 - sat) / oil_visc])


def mobility_slope(sat):
    return jnp.stack([2.0 * sat / water_visc, -2.0 * (1.0 - sat) / oil_visc])


def well_factors(sums, goal):
    return jnp.concatenate([((sums[1] - goal) / sums[0])[None], sums[2:] / sums[0][None]], axis=0)


def face_terms(trans, up, a, b, heads, ndir):
    pa, sa, vpa, vsa, wwa, woa = a
    pb, sb, vpb, vsb, wwb, wob = b
    su = jnp.where(up, sa, sb)
    drop = pa - pb
    pot_w = drop + heads[0]
    pot_o = drop + heads[1]
    tl_w = trans * (su * su / water_visc)
    tl_o = trans * ((1.0 - su) * (1.0 - su) / oil_visc)
    f_w = tl_w * pot_w
    f_o = tl_o * pot_o
    td_w = trans * (2.0 * su / water_visc) * pot_w
    td_o = trans * (-2.0 * (1.0 - su) / oil_visc) * pot_o
    jv_w, jv_o, jt_p, jt_s = [], [], [], []
    for d in range(ndir):
        vsu = jnp.where(up, vsa[d], vsb[d])
        dvp = vpa[d] - vpb[d]
        jv_w.append(td_w * vsu + tl_w * dvp)
        jv_o.append(td_o * vsu + tl_o * dvp)
        dww = wwa[d] - wwb[d]
        dwo = woa[d] - wob[d]
        jt_p.append(dww * tl_w + dwo * tl_o)
        jt_s.append(dww * td_w + dwo * td_o)
    zero = jnp.zeros_like(su)
    as_a = [f_w, f_o] + jv_w + jv_o + jt_p + [jnp.where(up, g, zero) for g in jt_s]
    as_b = [-f_w, -f_o] + [-x for x in jv_w] + [-x for x in jv_o] + [-x for x in jt_p]
    as_b = as_b + [jnp.where(up, zero, g) for g in jt_s]
    return as_a, as_b


def pack_kernel(p_ref, s_ref, d_ref, w_ref, tx_ref, ux_ref, ty_ref, uy_ref, xl_ref, xr_ref, yd_ref, yu_ref):
    ndir = d_ref.shape[0]
    layers, rows, cols = p_ref.shape
    lane = lax.broadcasted_iota(jnp.int32, (rows, cols), 1)
    sub = lax.broadcasted_iota(jnp.int32, (rows, cols), 0)
    nf = 2 + 4 * ndir

    def rolled(x, shift, axis):
        return x if shift == 0 else pltpu.roll(x, shift, axis)

    def rows_into(ref, k, tiles, source_row):
        count = len(tiles)
        for start in range(0, count, rows):
            acc = jnp.zeros((rows, cols), jnp.float32)
            for f in range(start, min(start + rows, count)):
                r = f - start
                acc = jnp.where(sub == r, rolled(tiles[f], (r - source_row) % rows, 0), acc)
            n = min(rows, count - start)
            ref[k, pl.ds(start, n), :] = acc[:n]

    def body(k, carry):
        cells = [p_ref[k], s_ref[k]]
        for half in range(2):
            cells += [d_ref[d, half, k] for d in range(ndir)]
        for half in range(2):
            cells += [w_ref[d, half, k] for d in range(ndir)]
        low_x = cells + [tx_ref[k], ux_ref[k].astype(jnp.float32)]
        low_y = cells + [ty_ref[k], uy_ref[k].astype(jnp.float32)]
        xl = jnp.zeros((rows, cols), jnp.float32)
        for f, t in enumerate(low_x):
            xl = jnp.where(lane == f, rolled(t, (f - (cols - 1)) % cols, 1), xl)
        xr = jnp.zeros((rows, cols), jnp.float32)
        for f, t in enumerate(cells):
            xr = jnp.where(lane == f, rolled(t, f % cols, 1), xr)
        xl_ref[k] = xl[:, : nf + 2]
        xr_ref[k] = xr[:, :nf]
        rows_into(yd_ref, k, low_y, rows - 1)
        rows_into(yu_ref, k, cells, 0)
        return carry

    lax.fori_loop(0, layers, body, 0)


def stencil_kernel(
    p_ref,
    s_ref,
    so_ref,
    pore_ref,
    tx_ref,
    ty_ref,
    tz_ref,
    ux_ref,
    uy_ref,
    uz_ref,
    d_ref,
    w_ref,
    pn_ref,
    sn_ref,
    dn_ref,
    wn_ref,
    hxl_ref,
    hxr_ref,
    hyd_ref,
    hyu_ref,
    r_out,
    jv_out,
    jt_out,
    carry_ref,
):
    ndir = d_ref.shape[0]
    span, rows, cols = p_ref.shape
    block = pl.program_id(0)
    layers = span * pl.num_programs(0)
    lane = lax.broadcasted_iota(jnp.int32, (rows, cols), 1)
    sub = lax.broadcasted_iota(jnp.int32, (rows, cols), 0)
    first_lane = lane == 0
    last_lane = lane == cols - 1
    first_sub = sub == 0
    last_sub = sub == rows - 1
    last_x = lax.axis_index("gx") == lax.axis_size("gx") - 1
    last_y = lax.axis_index(GY_WA) == lax.axis_size(GY_WA) - 1
    cut_x = jnp.logical_and(last_lane, last_x)
    cut_y = jnp.logical_and(last_sub, last_y)
    nf = 2 + 4 * ndir

    def cells_of(pr, sr, dr, wr, k):
        out = [pr[k], sr[k]]
        for half in range(2):
            out += [dr[d, half, k] for d in range(ndir)]
        for half in range(2):
            out += [wr[d, half, k] for d in range(ndir)]
        return out

    def group(flat):
        return (
            flat[0],
            flat[1],
            flat[2 : 2 + ndir],
            flat[2 + ndir : 2 + 2 * ndir],
            flat[2 + 2 * ndir : 2 + 3 * ndir],
            flat[2 + 3 * ndir : 2 + 4 * ndir],
        )

    def col(ref, k, f):
        return jnp.broadcast_to(ref[k, :, pl.ds(f, 1)], (rows, cols))

    def row(ref, k, f):
        return jnp.broadcast_to(ref[k, pl.ds(f, 1), :], (rows, cols))

    def store(k, vals):
        for i in range(nf):
            if i < 2:
                ref, idx = r_out, (i, k)
            elif i < 2 + 2 * ndir:
                j = i - 2
                ref, idx = jv_out, (j % ndir, j // ndir, k)
            else:
                j = i - 2 - 2 * ndir
                ref, idx = jt_out, (j % ndir, j // ndir, k)
            ref[idx] = vals[i]

    def layer(k, carry, above):
        here = cells_of(p_ref, s_ref, d_ref, w_ref, k)
        left = [jnp.where(first_lane, col(hxl_ref, k, f), pltpu.roll(x, 1, 1)) for f, x in enumerate(here)]
        right = [jnp.where(last_lane, col(hxr_ref, k, f), pltpu.roll(x, cols - 1, 1)) for f, x in enumerate(here)]
        down = [jnp.where(first_sub, row(hyd_ref, k, f), pltpu.roll(x, 1, 0)) for f, x in enumerate(here)]
        up_ = [jnp.where(last_sub, row(hyu_ref, k, f), pltpu.roll(x, rows - 1, 0)) for f, x in enumerate(here)]

        tx = tx_ref[k]
        ux = ux_ref[k].astype(jnp.float32)
        ty = ty_ref[k]
        uy = uy_ref[k].astype(jnp.float32)
        tx_f = jnp.where(cut_x, 0.0, tx)
        ty_f = jnp.where(cut_y, 0.0, ty)
        tx_b = jnp.where(first_lane, col(hxl_ref, k, nf), pltpu.roll(tx, 1, 1))
        ux_b = jnp.where(first_lane, col(hxl_ref, k, nf + 1), pltpu.roll(ux, 1, 1))
        ty_b = jnp.where(first_sub, row(hyd_ref, k, nf), pltpu.roll(ty, 1, 0))
        uy_b = jnp.where(first_sub, row(hyd_ref, k, nf + 1), pltpu.roll(uy, 1, 0))
        tz = jnp.where(block * span + k < layers - 1, tz_ref[k], 0.0)
        uz = uz_ref[k] == 1

        g_here = group(here)
        acc, _ = face_terms(tx_f, ux > 0.5, g_here, group(right), (0.0, 0.0), ndir)
        _, xb = face_terms(tx_b, ux_b > 0.5, group(left), g_here, (0.0, 0.0), ndir)
        yf, _ = face_terms(ty_f, uy > 0.5, g_here, group(up_), (0.0, 0.0), ndir)
        _, yb = face_terms(ty_b, uy_b > 0.5, group(down), g_here, (0.0, 0.0), ndir)
        zf, zb = face_terms(tz, uz, g_here, group(above), (water_head, oil_head), ndir)
        acc = [a + b + c + e for a, b, c, e in zip(acc, xb, yf, yb)]
        acc = [a + z for a, z in zip(acc, zf)]

        change = here[1] - so_ref[k]
        pore = pore_ref[k]
        acc[0] = acc[0] + pore * change
        acc[1] = acc[1] - pore * change
        for d in range(ndir):
            vs = here[2 + ndir + d]
            acc[2 + d] = acc[2 + d] + pore * vs
            acc[2 + ndir + d] = acc[2 + ndir + d] - pore * vs
            jt_s = 2 + 3 * ndir + d
            acc[jt_s] = acc[jt_s] + pore * (here[2 + 2 * ndir + d] - here[2 + 3 * ndir + d])
        acc = [a + c for a, c in zip(acc, carry)]
        store(k, acc)
        return tuple(zb)

    @pl.when(block == 0)
    def _():
        carry_ref[...] = jnp.zeros_like(carry_ref)

    def inner(k, carry):
        return layer(k, carry, cells_of(p_ref, s_ref, d_ref, w_ref, k + 1))

    carry = tuple(carry_ref[i] for i in range(nf))
    carry = lax.fori_loop(0, span - 1, inner, carry)
    carry = layer(span - 1, carry, cells_of(pn_ref, sn_ref, dn_ref, wn_ref, 0))
    for i in range(nf):
        carry_ref[i] = carry[i]


def layer_body(
    pressure,
    saturation,
    sat_old,
    pore,
    trans_x,
    trans_y,
    trans_z,
    upwind_x,
    upwind_y,
    upwind_z,
    directions,
    adjoint_weights,
    perf_well,
    perf_col,
    perf_top,
    perf_span,
    perf_index,
    bhp,
    target,
):
    layers, rows, cols = pressure.shape
    spatial = (layers, rows, cols)
    ndir = directions.shape[0]

    nf = 2 + 4 * ndir
    vmem = pl.BlockSpec(memory_space=pltpu.VMEM)
    x_low, x_high, y_low, y_high = pl.pallas_call(
        pack_kernel,
        out_shape=[
            jax.ShapeDtypeStruct((layers, rows, nf + 2), jnp.float32),
            jax.ShapeDtypeStruct((layers, rows, nf), jnp.float32),
            jax.ShapeDtypeStruct((layers, nf + 2, cols), jnp.float32),
            jax.ShapeDtypeStruct((layers, nf, cols), jnp.float32),
        ],
        in_specs=[vmem] * 8,
        out_specs=[vmem] * 4,
        cost_estimate=pl.CostEstimate(
            flops=layers * rows * cols * 160,
            transcendentals=0,
            bytes_accessed=(6 + 4 * ndir) * layers * rows * cols * 4,
        ),
    )(pressure, saturation, directions, adjoint_weights, trans_x, upwind_x, trans_y, upwind_y)
    x_low, x_high, y_low, y_high, pressure, saturation, directions, adjoint_weights = lax.optimization_barrier(
        (x_low, x_high, y_low, y_high, pressure, saturation, directions, adjoint_weights)
    )
    hxl = shift_along(x_low, "gx", True)
    hxr = shift_along(x_high, "gx", False)
    hyd = shift_along(y_low, GY_WA, True)
    hyu = shift_along(y_high, GY_WA, False)

    lane_hit = (jnp.arange(cols)[:, None] == (perf_col % cols)[None, :]).astype(jnp.float32)
    row_hit = (jnp.arange(rows)[:, None] == (perf_col // cols)[None, :]).astype(jnp.float32)

    def at_perfs(field):
        by_lane = jnp.dot(field, lane_hit, precision=lax.Precision.HIGHEST)
        return jnp.sum(by_lane * row_hit, axis=-2)

    p_cells = at_perfs(pressure)
    s_cells = at_perfs(saturation)
    dir_cells = at_perfs(directions)
    wts_cells = at_perfs(adjoint_weights)
    depth = jnp.arange(layers)[:, None]
    open_layer = jnp.logical_and(
        depth >= perf_top[None, :], depth < (perf_top + perf_span)[None, :]
    )
    weight = jnp.where(open_layer, perf_index[None, :], 0.0)
    row_bhp, row_target = jnp.take(jnp.stack([bhp, target]), perf_well, axis=1)
    drive = p_cells - row_bhp
    mob = mobility(s_cells)
    slope = mobility_slope(s_cells)
    mob_total = mob[0] + mob[1]
    slope_total = slope[0] + slope[1]
    rates = weight * mob * drive
    rate_tangent = weight * (mob * dir_cells[:, 0:1] + slope * drive * dir_cells[:, 1:2])
    grad_p = weight * (mob[0] * wts_cells[:, 0] + mob[1] * wts_cells[:, 1])
    grad_s = weight * drive * (slope[0] * wts_cells[:, 0] + slope[1] * wts_cells[:, 1])
    row_sums = jnp.concatenate(
        [
            jnp.sum(weight * mob_total, axis=0)[None],
            jnp.sum(rates[0] + rates[1], axis=0)[None],
            jnp.sum(rate_tangent[:, 0] + rate_tangent[:, 1], axis=1),
            jnp.sum(grad_p, axis=1),
        ],
        axis=0,
    )
    packed = jnp.concatenate([row_sums, perf_well.astype(jnp.float32)[None]], axis=0)
    everyone = gather_everywhere(packed)


    all_sums = jnp.moveaxis(everyone[:, :-1], 1, 0).reshape(row_sums.shape[0], -1)
    all_wells = everyone[:, -1].reshape(-1)
    same_well = (perf_well.astype(jnp.float32)[:, None] == all_wells[None, :]).astype(jnp.float32)
    row_totals = jnp.dot(all_sums, same_well.T, precision=lax.Precision.HIGHEST)
    row_factors = well_factors(row_totals, row_target)
    wells_res = rates - weight * mob * row_factors[0]
    wells_fwd = rate_tangent - (weight * mob)[None] * row_factors[1 : 1 + ndir][:, None, None, :]
    out_f = row_factors[1 + ndir :][:, None, :]
    wells_adj = jnp.stack(
        [grad_p - weight * mob_total * out_f, grad_s - weight * slope_total * drive * out_f], axis=1
    )
    combined = jnp.concatenate([wells_res[None], wells_fwd, wells_adj], axis=0)
    by_row = combined[..., None, :] * row_hit
    spread = jnp.dot(by_row, lane_hit.T, precision=lax.Precision.HIGHEST)

    span = 6 if layers % 6 == 0 else layers
    blocks = layers // span

    def layer_block(*lead):
        return pl.BlockSpec(tuple(lead) + (span, rows, cols), lambda b: (0,) * len(lead) + (b, 0, 0))

    def next_layer(*lead):
        return pl.BlockSpec(
            tuple(lead) + (1, rows, cols),
            lambda b: (0,) * len(lead) + (jnp.minimum((b + 1) * span, layers - 1), 0, 0),
        )

    def halo_block(mid, last):
        return pl.BlockSpec((span, mid, last), lambda b: (b, 0, 0))

    flux = pl.pallas_call(
        stencil_kernel,
        grid=(blocks,),
        out_shape=[
            jax.ShapeDtypeStruct((2,) + spatial, jnp.float32),
            jax.ShapeDtypeStruct((ndir, 2) + spatial, jnp.float32),
            jax.ShapeDtypeStruct((ndir, 2) + spatial, jnp.float32),
        ],
        in_specs=[layer_block()] * 10
        + [layer_block(ndir, 2)] * 2
        + [next_layer()] * 2
        + [next_layer(ndir, 2)] * 2
        + [
            halo_block(rows, nf + 2),
            halo_block(rows, nf),
            halo_block(nf + 2, cols),
            halo_block(nf, cols),
        ],
        out_specs=[layer_block(2), layer_block(ndir, 2), layer_block(ndir, 2)],
        scratch_shapes=[pltpu.VMEM((nf, rows, cols), jnp.float32)],
        compiler_params=pltpu.CompilerParams(dimension_semantics=("arbitrary",)),
        cost_estimate=pl.CostEstimate(
            flops=layers * rows * cols * 1200,
            transcendentals=0,
            bytes_accessed=(10 + 4 * 4 * ndir + 2 + 2 * 2 * ndir) * layers * rows * cols * 4,
        ),
    )(
        pressure,
        saturation,
        sat_old,
        pore,
        trans_x,
        trans_y,
        trans_z,
        upwind_x,
        upwind_y,
        upwind_z,
        directions,
        adjoint_weights,
        pressure,
        saturation,
        directions,
        adjoint_weights,
        hxl,
        hxr,
        hyd,
        hyu,
    )
    reduced_residual, forward_products, adjoint_products = flux
    reduced_residual = reduced_residual + spread[0]
    forward_products = forward_products + spread[1 : 1 + ndir]
    adjoint_products = adjoint_products + spread[1 + ndir :]
    return (reduced_residual, forward_products, adjoint_products)


def solution(mesh):
    split = Mesh(
        mesh.devices.reshape(mesh.shape["gx"], 4, 4, mesh.shape["wa"]), ("gx", "gy_0", "gy_1", "wa")
    )
    return jax.shard_map(
        layer_body,
        mesh=split,
        in_specs=(
            P(None, GY_WA, "gx"),
            P(None, GY_WA, "gx"),
            P(None, GY_WA, "gx"),
            P(None, GY_WA, "gx"),
            P(None, GY_WA, "gx"),
            P(None, GY_WA, "gx"),
            P(None, GY_WA, "gx"),
            P(None, GY_WA, "gx"),
            P(None, GY_WA, "gx"),
            P(None, GY_WA, "gx"),
            P(None, None, None, GY_WA, "gx"),
            P(None, None, None, GY_WA, "gx"),
            P(GX_GY_WA),
            P(GX_GY_WA),
            P(GX_GY_WA),
            P(GX_GY_WA),
            P(GX_GY_WA),
            P(),
            P(),
        ),
        out_specs=(
            P(None, None, GY_WA, "gx"),
            P(None, None, None, GY_WA, "gx"),
            P(None, None, None, GY_WA, "gx"),
        ),
        check_vma=False,
    )
```

profile of v0, /device:TPU:27, one launch (start us, length us, event | category | flops | bytes accessed | tf_op | source)
XLA Modules:
  0.0 55.1 jit_solution(7744940578176726340)
XLA Ops:
  0.7 0.8 %compare_and_fusion = pred[32]{0:T(512)(128)(4,1)S(1)} fusion(s32[32]{0:T(128)} %param.31), kind=kLoop, calls=%fused_computation.70 | loop fusion | flops 192 | bytes 160 | tf_op jit(solution)/shard_map/jit(_take)/and | solution.py:321
  1.5 0.7 %fusion.44 = (f32[32]{0:T(128)S(1)}, f32[1,32]{1,0:T(1,128)S(1)}, s32[32]{0:T(128)S(1)}) fusion(s32[32]{0:T(128)} %param.31), kind=kLoop, calls=%fused_computation.91 | loop fusion | flops 128 | bytes 512 | tf_op jit(solution)/shard_map/convert_element_type | solution.py:340
  2.2 0.7 %and_select_fusion.1 = (s32[32]{0:T(128)S(1)}, s32[32]{0:T(128)S(1)}) fusion(s32[32]{0:T(128)} %param.32), kind=kLoop, calls=%fused_computation.72 | loop fusion | flops 608 | bytes 384 | tf_op jit(solution)/shard_map/jit(remainder)/select_n | solution.py:305
  2.9 4.9 %shard_map.202 = (f32[24,8,20]{2,1,0:T(8,128)}, f32[24,8,18]{2,1,0:T(8,128)}, f32[24,20,128]{2,1,0:T(8,128)}, f32[24,18,128]{2,1,0:T(8,128)}) custom-call(f32[24,8,128]{2,1,0:T(8,128)} %pn_ref, f32[24,8,128]{2,1,0:T(8,128)} %sn_ref, f32[4,2,24,8,128]{4,3,2,1,0:T(8,128)} %dn_ref, f32[4,2,24,8,128]{4,3,2,1,0:T(8,128)} %wn_ref, f32[24,8,128]{2,1,0:T(8,128)} %tx_ref.3, ...), custom_call_target="tpu_custom_call" | custom-call | flops 3932160 | bytes 2162688 | tf_op jit(solution)/shard_map/pallas_call | solution.py:281
  7.9 0.3 fusion.5
  8.5 0.7 %fusion.3 = f32[4,2,24,32]{3,2,1,0:T(8,128)S(1)} fusion(f32[4,2,24,8,128]{4,3,2,1,0:T(8,128)S(1)} %copy-done.1, f32[8,32]{1,0:T(8,128)S(1)} %fusion.33, s32[32]{0:T(128)S(1)} %get-tuple-element.67), kind=kOutput, calls=%fused_computation.6 | convolution fusion | flops 75593728 | bytes 812160 | tf_op jit(solution)/shard_map/dot_general | solution.py:309
  9.2 0.7 %fusion.2 = f32[4,2,24,32]{3,2,1,0:T(8,128)S(1)} fusion(f32[4,2,24,8,128]{4,3,2,1,0:T(8,128)S(1)} %copy-done, f32[8,32]{1,0:T(8,128)S(1)} %fusion.33, s32[32]{0:T(128)S(1)} %get-tuple-element.67), kind=kOutput, calls=%fused_computation.5 | convolution fusion | flops 75593728 | bytes 812160 | tf_op jit(solution)/shard_map/dot_general | solution.py:309
  9.9 0.4 copy.28
  10.3 0.6 %gather_fusion = f32[32,2]{1,0:T(8,128)S(1)} fusion(f32[2,2048]{0,1:T(8,128)S(1)} %copy.28, s32[1024]{0:T(1024)S(1)} %pad_clamp_fusion), kind=kCustom, calls=%fused_computation | custom fusion | bytes 640 | tf_op jit(solution)/shard_map/jit(_take)/gather | solution.py:321
  11.4 0.8 %broadcast_in_dim.43 = f32[128,1,352]{2,1,0:T(1,128)} broadcast(f32[352]{0:T(512)S(1)} %broadcast_in_dim.42), dimensions={2} | broadcast | bytes 181632 | tf_op jit(solution)/shard_map/broadcast_in_dim | solution.py:22
  12.2 10.5 %all-to-all-start = ((f32[128,1,352]{2,1,0:T(1,128)}), f32[128,1,352]{2,1,0:T(1,128)S(1)}, u32[]{:S(2)}, u32[]{:S(2)}) async-start(f32[128,1,352]{2,1,0:T(1,128)} %broadcast_in_dim.43), calls=%async_computation | async-start | bytes 393216 | tf_op jit(solution)/shard_map/all_to_all | solution.py:23
  22.7 3.1 %collective-permute-start = (f32[24,8,20]{2,1,0:T(8,128)S(1)}, f32[24,8,20]{2,1,0:T(8,128)S(1)}, u32[]{:S(2)}, u32[]{:S(2)}) collective-permute-start(f32[24,8,20]{2,1,0:T(8,128)S(1)} %copy-done.14), channel_id=1, source_target_pairs={{0,32},{32,64},{64,96},{1,33},{33,65},{65,97},{2,34},{34,66},{66,9... | collective-permute-start | bytes 46088 | tf_op jit(solution)/shard_map/ppermute | solution.py:31
  25.9 2.2 %collective-permute-start.1 = (f32[24,8,18]{2,1,0:T(8,128)S(1)}, f32[24,8,18]{2,1,0:T(8,128)S(1)}, u32[]{:S(2)}, u32[]{:S(2)}) collective-permute-start(f32[24,8,18]{2,1,0:T(8,128)S(1)} %copy-done.15), channel_id=1, source_target_pairs={{32,0},{64,32},{96,64},{33,1},{65,33},{97,65},{34,2},{66,34},{98,6... | collective-permute-start | bytes 41480 | tf_op jit(solution)/shard_map/ppermute | solution.py:31
  28.1 4.0 %collective-permute-start.2 = (f32[24,20,128]{2,1,0:T(8,128)S(1)}, f32[24,20,128]{2,1,0:T(8,128)S(1)}, u32[]{:S(2)}, u32[]{:S(2)}) collective-permute-start(f32[24,20,128]{2,1,0:T(8,128)S(1)} %copy-done.12), channel_id=1, source_target_pairs={{0,1},{1,2},{2,3},{3,4},{4,5},{5,6},{6,7},{7,8},{8,9},{9,10},{10,1... | collective-permute-start | bytes 737288 | tf_op jit(solution)/shard_map/ppermute | solution.py:31
  32.1 1.9 %collective-permute-start.3 = (f32[24,18,128]{2,1,0:T(8,128)S(1)}, f32[24,18,128]{2,1,0:T(8,128)S(1)}, u32[]{:S(2)}, u32[]{:S(2)}) collective-permute-start(f32[24,18,128]{2,1,0:T(8,128)S(1)} %copy-done.13), channel_id=1, source_target_pairs={{1,0},{2,1},{3,2},{4,3},{5,4},{6,5},{7,6},{8,7},{9,8},{10,9},{11,1... | collective-permute-start | bytes 663560 | tf_op jit(solution)/shard_map/ppermute | solution.py:31
  34.6 0.3 reshape.530
  34.9 0.4 fusion.8
  35.5 1.0 %fusion = f32[9,2,24,8,128]{4,3,2,1,0:T(8,128)S(1)} fusion(f32[8,32]{1,0:T(8,128)S(1)} %fusion.33, f32[9,2,24,32]{3,2,1,0:T(8,128)S(1)} %maximum_maximum_fusion, s32[32]{0:T(128)S(1)} %get-tuple-element.67), kind=kOutput, calls=%fused_computation.1 | convolution fusion | flops 169984000 | bytes 1825920 | tf_op jit(solution)/shard_map/dot_general | solution.py:357
  36.6 5.6 %collective-permute-done.3.hyu_ref = f32[24,18,128]{2,1,0:T(8,128)S(1)} collective-permute-done((f32[24,18,128]{2,1,0:T(8,128)S(1)}, f32[24,18,128]{2,1,0:T(8,128)S(1)}, u32[]{:S(2)}, u32[]{:S(2)}) %collective-permute-start.3) | collective-permute-done | bytes 221216 | tf_op jit(solution)/shard_map/ppermute | solution.py:31
  42.2 0.7 %copy-done.5 = f32[24,18,128]{2,1,0:T(8,128)} copy-done((f32[24,18,128]{2,1,0:T(8,128)}, f32[24,18,128]{2,1,0:T(8,128)S(1)}, u32[]{:S(2)}) %copy-start.5) | copy-done | bytes 221208
  43.0 0.7 %copy-done.4 = f32[24,20,128]{2,1,0:T(8,128)} copy-done((f32[24,20,128]{2,1,0:T(8,128)}, f32[24,20,128]{2,1,0:T(8,128)S(1)}, u32[]{:S(2)}) %copy-start.4) | copy-done | bytes 245784
  43.7 7.1 %shard_map.203 = (f32[2,24,8,128]{3,2,1,0:T(8,128)}, f32[4,2,24,8,128]{4,3,2,1,0:T(8,128)}, f32[4,2,24,8,128]{4,3,2,1,0:T(8,128)}) custom-call(f32[24,8,128]{2,1,0:T(8,128)} %pn_ref, f32[24,8,128]{2,1,0:T(8,128)} %sn_ref, f32[24,8,128]{2,1,0:T(8,128)} %so_ref.1, f32[24,8,128]{2,1,0:T(8,128)} %pore_ref.1, f32[24,8,128]{2,1,0:T(8,128)} %tx_ref.3, ...), custom_call_target="tpu_custom_call" | custom-call | flops 29491200 | bytes 9043968 | tf_op jit(solution)/shard_map/pallas_call | solution.py:374
  50.8 1.6 %fusion.12 = f32[2,24,8,128]{3,2,1,0:T(8,128)} fusion(f32[2,24,8,128]{3,2,1,0:T(8,128)} %get-tuple-element.30, f32[9,2,24,8,128]{4,3,2,1,0:T(8,128)S(1)} %fusion), kind=kLoop, calls=%fused_computation.21 | loop fusion | flops 49152 | bytes 589824 | tf_op jit(solution)/shard_map/add | solution.py:423
  52.4 2.7 %slice_add_fusion = (f32[4,2,24,8,128]{4,3,2,1,0:T(8,128)}, f32[4,2,24,8,128]{4,3,2,1,0:T(8,128)}) fusion(f32[4,2,24,8,128]{4,3,2,1,0:T(8,128)} %get-tuple-element.32, f32[9,2,24,8,128]{4,3,2,1,0:T(8,128)S(1)} %fusion, f32[4,2,24,8,128]{4,3,2,1,0:T(8,128)} %get-tuple-element.31), kind=kLoop, calls=%fused_computation.13 | loop fusion | flops 393216 | bytes 4718592 | tf_op jit(solution)/shard_map/add | solution.py:425
  (68 shorter events, 1.5 us)
Async XLA Ops:
  0.6 7.8 %copy-start.1 = (f32[4,2,24,8,128]{4,3,2,1,0:T(8,128)S(1)}, f32[4,2,24,8,128]{4,3,2,1,0:T(8,128)}, u32[]{:S(2)}) copy-start(f32[4,2,24,8,128]{4,3,2,1,0:T(8,128)} %wn_ref) | copy-start | bytes 2359300
  0.6 8.5 %copy-start = (f32[4,2,24,8,128]{4,3,2,1,0:T(8,128)S(1)}, f32[4,2,24,8,128]{4,3,2,1,0:T(8,128)}, u32[]{:S(2)}) copy-start(f32[4,2,24,8,128]{4,3,2,1,0:T(8,128)} %dn_ref) | copy-start | bytes 2359300
  0.7 7.5 %copy-start.3 = (f32[24,8,128]{2,1,0:T(8,128)S(1)}, f32[24,8,128]{2,1,0:T(8,128)}, u32[]{:S(2)}) copy-start(f32[24,8,128]{2,1,0:T(8,128)} %sn_ref) | copy-start | bytes 294916
  0.7 7.2 %copy-start.2 = (f32[24,8,128]{2,1,0:T(8,128)S(1)}, f32[24,8,128]{2,1,0:T(8,128)}, u32[]{:S(2)}) copy-start(f32[24,8,128]{2,1,0:T(8,128)} %pn_ref) | copy-start | bytes 294916
  2.9 7.0 %copy-start.8 = (f32[2048]{0:T(1024)S(1)}, f32[2048]{0:T(1024)}, u32[]{:S(2)}) copy-start(f32[2048]{0:T(1024)} %param.37) | copy-start | bytes 24580
  2.9 7.0 %copy-start.9 = (f32[2048]{0:T(1024)S(1)}, f32[2048]{0:T(1024)}, u32[]{:S(2)}) copy-start(f32[2048]{0:T(1024)} %param.36) | copy-start | bytes 24580
  7.9 3.1 %copy-start.11 = (s32[32]{0:T(128)S(1)}, s32[32]{0:T(128)}, u32[]{:S(2)}) copy-start(s32[32]{0:T(128)} %param.33) | copy-start | bytes 388
  7.9 3.1 %copy-start.16 = (s32[32]{0:T(128)S(1)}, s32[32]{0:T(128)}, u32[]{:S(2)}) copy-start(s32[32]{0:T(128)} %param.34) | copy-start | bytes 388
  7.9 3.1 %copy-start.10 = (f32[32]{0:T(128)S(1)}, f32[32]{0:T(128)}, u32[]{:S(2)}) copy-start(f32[32]{0:T(128)} %param.35) | copy-start | bytes 388
  9.2 13.6 %copy-start.14 = (f32[24,8,20]{2,1,0:T(8,128)S(1)}, f32[24,8,20]{2,1,0:T(8,128)}, u32[]{:S(2)}) copy-start(f32[24,8,20]{2,1,0:T(8,128)} %get-tuple-element.26) | copy-start | bytes 46084
  9.2 16.7 %copy-start.15 = (f32[24,8,18]{2,1,0:T(8,128)S(1)}, f32[24,8,18]{2,1,0:T(8,128)}, u32[]{:S(2)}) copy-start(f32[24,8,18]{2,1,0:T(8,128)} %get-tuple-element.27) | copy-start | bytes 41476
  9.2 18.9 %copy-start.12 = (f32[24,20,128]{2,1,0:T(8,128)S(1)}, f32[24,20,128]{2,1,0:T(8,128)}, u32[]{:S(2)}) copy-start(f32[24,20,128]{2,1,0:T(8,128)} %get-tuple-element.28) | copy-start | bytes 737284
  9.2 22.9 %copy-start.13 = (f32[24,18,128]{2,1,0:T(8,128)S(1)}, f32[24,18,128]{2,1,0:T(8,128)}, u32[]{:S(2)}) copy-start(f32[24,18,128]{2,1,0:T(8,128)} %get-tuple-element.29) | copy-start | bytes 663556
  12.2 21.8 %all-to-all-start = ((f32[128,1,352]{2,1,0:T(1,128)}), f32[128,1,352]{2,1,0:T(1,128)S(1)}, u32[]{:S(2)}, u32[]{:S(2)}) async-start(f32[128,1,352]{2,1,0:T(1,128)} %broadcast_in_dim.43), calls=%async_computation | async-start | bytes 393216 | tf_op jit(solution)/shard_map/all_to_all | solution.py:23
  22.7 13.8 %collective-permute-start = (f32[24,8,20]{2,1,0:T(8,128)S(1)}, f32[24,8,20]{2,1,0:T(8,128)S(1)}, u32[]{:S(2)}, u32[]{:S(2)}) collective-permute-start(f32[24,8,20]{2,1,0:T(8,128)S(1)} %copy-done.14), channel_id=1, source_target_pairs={{0,32},{32,64},{64,96},{1,33},{33,65},{65,97},{2,34},{34,66},{66,9... | collective-permute-start | bytes 46088 | tf_op jit(solution)/shard_map/ppermute | solution.py:31
  25.9 10.7 %collective-permute-start.1 = (f32[24,8,18]{2,1,0:T(8,128)S(1)}, f32[24,8,18]{2,1,0:T(8,128)S(1)}, u32[]{:S(2)}, u32[]{:S(2)}) collective-permute-start(f32[24,8,18]{2,1,0:T(8,128)S(1)} %copy-done.15), channel_id=1, source_target_pairs={{32,0},{64,32},{96,64},{33,1},{65,33},{97,65},{34,2},{66,34},{98,6... | collective-permute-start | bytes 41480 | tf_op jit(solution)/shard_map/ppermute | solution.py:31
  28.1 14.2 %collective-permute-start.2 = (f32[24,20,128]{2,1,0:T(8,128)S(1)}, f32[24,20,128]{2,1,0:T(8,128)S(1)}, u32[]{:S(2)}, u32[]{:S(2)}) collective-permute-start(f32[24,20,128]{2,1,0:T(8,128)S(1)} %copy-done.12), channel_id=1, source_target_pairs={{0,1},{1,2},{2,3},{3,4},{4,5},{5,6},{6,7},{7,8},{8,9},{9,10},{10,1... | collective-permute-start | bytes 737288 | tf_op jit(solution)/shard_map/ppermute | solution.py:31
  32.1 10.2 %collective-permute-start.3 = (f32[24,18,128]{2,1,0:T(8,128)S(1)}, f32[24,18,128]{2,1,0:T(8,128)S(1)}, u32[]{:S(2)}, u32[]{:S(2)}) collective-permute-start(f32[24,18,128]{2,1,0:T(8,128)S(1)} %copy-done.13), channel_id=1, source_target_pairs={{1,0},{2,1},{3,2},{4,3},{5,4},{6,5},{7,6},{8,7},{9,8},{10,9},{11,1... | collective-permute-start | bytes 663560 | tf_op jit(solution)/shard_map/ppermute | solution.py:31
  36.6 5.7 %copy-start.7 = (f32[24,8,18]{2,1,0:T(8,128)}, f32[24,8,18]{2,1,0:T(8,128)S(1)}, u32[]{:S(2)}) copy-start(f32[24,8,18]{2,1,0:T(8,128)S(1)} %collective-permute-done.1.hxr_ref) | copy-start | bytes 41476
  36.6 5.6 %copy-start.6 = (f32[24,8,20]{2,1,0:T(8,128)}, f32[24,8,20]{2,1,0:T(8,128)S(1)}, u32[]{:S(2)}) copy-start(f32[24,8,20]{2,1,0:T(8,128)S(1)} %collective-permute-done.hxl_ref) | copy-start | bytes 46084
  42.2 0.7 %copy-start.5 = (f32[24,18,128]{2,1,0:T(8,128)}, f32[24,18,128]{2,1,0:T(8,128)S(1)}, u32[]{:S(2)}) copy-start(f32[24,18,128]{2,1,0:T(8,128)S(1)} %collective-permute-done.3.hyu_ref) | copy-start | bytes 663556
  43.0 0.7 %copy-start.4 = (f32[24,20,128]{2,1,0:T(8,128)}, f32[24,20,128]{2,1,0:T(8,128)S(1)}, u32[]{:S(2)}) copy-start(f32[24,20,128]{2,1,0:T(8,128)S(1)} %collective-permute-done.2.hyd_ref) | copy-start | bytes 737284
where the time goes:
time: 55.5 us; the launch traced here: 55.1 us
  starting transfers between devices  21.7 us (39%)
  Pallas kernels  12.1 us (22%)
  other arithmetic  6.82 us (12%)
  waiting for transfers between devices  5.63 us (10%)
  local copies, waits for them, and re-layouts  4.41 us (8%)
  matrix products  3.34 us (6%)
  between operations  1.1 us (2%)
    ppermute x4, starting transfers between devices, shift_along(): return lax.ppermute(block, axis, pairs)  11.2 us
    all_to_all x1, starting transfers between devices, gather_everywhere(): lax.all_to_all(flat, GX_GY_WA, 0, 0, tiled=True)  10.5 us
    pallas_call x1, Pallas kernels, layer_body(): pl.pallas_call(stencil_kernel, grid=(blocks,), out_shape=[jax.ShapeDtypeS...  7.14 us
    ppermute x4, waiting for transfers between devices, shift_along(): return lax.ppermute(block, axis, pairs)  5.63 us
    pallas_call x1, Pallas kernels, layer_body(): pl.pallas_call(pack_kernel, out_shape=[jax.ShapeDtypeStruct((layers, rows...  4.93 us
    add x1, other arithmetic, layer_body(): adjoint_products = adjoint_products + spread[1 + ndir:]  2.67 us
    dot_general x4, matrix products, at_perfs(): by_lane = jnp.dot(field, lane_hit, precision=lax.Precision.HIGHEST)  1.88 us
    add x1, other arithmetic, layer_body(): reduced_residual = reduced_residual + spread[0]  1.63 us
  transfers between devices with their start and end apart: 5, of which 1 were waited for; matrix products, arithmetic and copies ran while one was open for 4% of the time, Pallas kernels for 0%

commit v1 on v0

--- a/solution.py
+++ b/solution.py
@@ -278,7 +278,7 @@
 
     nf = 2 + 4 * ndir
     vmem = pl.BlockSpec(memory_space=pltpu.VMEM)
-    x_low, x_high, y_low, y_high = pl.pallas_call(
+    packs = pl.pallas_call(
         pack_kernel,
         out_shape=[
             jax.ShapeDtypeStruct((layers, rows, nf + 2), jnp.float32),
@@ -294,9 +294,7 @@
             bytes_accessed=(6 + 4 * ndir) * layers * rows * cols * 4,
         ),
     )(pressure, saturation, directions, adjoint_weights, trans_x, upwind_x, trans_y, upwind_y)
-    x_low, x_high, y_low, y_high, pressure, saturation, directions, adjoint_weights = lax.optimization_barrier(
-        (x_low, x_high, y_low, y_high, pressure, saturation, directions, adjoint_weights)
-    )
+    x_low, x_high, y_low, y_high = packs
     hxl = shift_along(x_low, "gx", True)
     hxr = shift_along(x_high, "gx", False)
     hyd = shift_along(y_low, GY_WA, True)

time: 55.5 us -> 59.4 us (1.070)
  matrix products: 3.34 us -> 7.16 us
    dot_general x4, matrix products: 1.88 us -> 5.71 us  [at_perfs(): by_lane = jnp.dot(field, lane_hit, precision=lax.Precision.HIGHEST)]
    unnamed x34 -> x18, local copies, waits for them, and re-layouts: 1.5 us -> 1.42 us
  transfers between devices with their start and end apart: 5 -> 5, of which waited for: 1 -> 1; matrix products, arithmetic and copies ran while one was open for 4% -> 4% of each run, Pallas kernels for 0% -> 8%
where the time goes in v1:
time: 59.4 us; the launch traced here: 58.8 us
  starting transfers between devices  21.7 us (37%)
  Pallas kernels  12.1 us (20%)
  matrix products  7.16 us (12%)
  other arithmetic  6.69 us (11%)
  waiting for transfers between devices  5.84 us (10%)
  local copies, waits for them, and re-layouts  4.33 us (7%)
  between operations  0.99 us (2%)
    ppermute x4, starting transfers between devices, shift_along(): return lax.ppermute(block, axis, pairs)  11.2 us
    all_to_all x1, starting transfers between devices, gather_everywhere(): lax.all_to_all(flat, GX_GY_WA, 0, 0, tiled=True)  10.5 us
    pallas_call x1, Pallas kernels, layer_body(): pl.pallas_call(stencil_kernel, grid=(blocks,), out_shape=[jax.ShapeDtypeS...  7.14 us
    ppermute x4, waiting for transfers between devices, shift_along(): return lax.ppermute(block, axis, pairs)  5.84 us
    dot_general x4, matrix products, at_perfs(): by_lane = jnp.dot(field, lane_hit, precision=lax.Precision.HIGHEST)  5.71 us
    pallas_call x1, Pallas kernels, layer_body(): pl.pallas_call(pack_kernel, out_shape=[jax.ShapeDtypeStruct((layers, rows...  4.93 us
    add x1, other arithmetic, layer_body(): adjoint_products = adjoint_products + spread[1 + ndir:]  2.67 us
    add x1, other arithmetic, layer_body(): reduced_residual = reduced_residual + spread[0]  1.63 us
  transfers between devices with their start and end apart: 5, of which 1 were waited for; matrix products, arithmetic and copies ran while one was open for 4% of the time, Pallas kernels for 8%

profile of v1, /device:TPU:27, one launch (start us, length us, event | category | flops | bytes accessed | tf_op | source)
XLA Modules:
  0.0 58.8 jit_solution(8838655285969062630)
XLA Ops:
  0.7 0.7 %compare_and_fusion = pred[32]{0:T(512)(128)(4,1)S(1)} fusion(s32[32]{0:T(128)} %param.31), kind=kLoop, calls=%fused_computation.78 | loop fusion | flops 192 | bytes 160 | tf_op jit(solution)/shard_map/jit(_take)/and | solution.py:319
  1.4 0.7 %fusion.52 = (f32[32]{0:T(128)S(1)}, f32[1,32]{1,0:T(1,128)S(1)}, s32[32]{0:T(128)S(1)}) fusion(s32[32]{0:T(128)} %param.31), kind=kLoop, calls=%fused_computation.99 | loop fusion | flops 128 | bytes 512 | tf_op jit(solution)/shard_map/convert_element_type | solution.py:338
  2.1 0.7 %and_select_fusion.1 = (s32[32]{0:T(128)S(1)}, s32[32]{0:T(128)S(1)}) fusion(s32[32]{0:T(128)} %param.32), kind=kLoop, calls=%fused_computation.80 | loop fusion | flops 608 | bytes 384 | tf_op jit(solution)/shard_map/jit(remainder)/select_n | solution.py:303
  2.8 1.1 %fusion.9 = f32[24,32]{1,0:T(8,128)S(1)} fusion(f32[24,8,128]{2,1,0:T(8,128)} %pn_ref.1, f32[8,32]{1,0:T(8,128)S(1)} %fusion.41, s32[32]{0:T(128)S(1)} %get-tuple-element.51), kind=kOutput, calls=%fused_computation.14 | convolution fusion | flops 9452800 | bytes 102528 | tf_op jit(solution)/shard_map/dot_general | solution.py:307
  3.9 1.1 %fusion.8 = f32[24,32]{1,0:T(8,128)S(1)} fusion(f32[24,8,128]{2,1,0:T(8,128)} %sn_ref.1, f32[8,32]{1,0:T(8,128)S(1)} %fusion.41, s32[32]{0:T(128)S(1)} %get-tuple-element.51), kind=kOutput, calls=%fused_computation.13 | convolution fusion | flops 9452800 | bytes 102528 | tf_op jit(solution)/shard_map/dot_general | solution.py:307
  5.1 1.7 %fusion.5 = f32[4,2,24,32]{3,2,1,0:T(8,128)S(1)} fusion(f32[4,2,24,8,128]{4,3,2,1,0:T(8,128)} %wn_ref.1, f32[8,32]{1,0:T(8,128)S(1)} %fusion.41, s32[32]{0:T(128)S(1)} %get-tuple-element.51), kind=kOutput, calls=%fused_computation.8 | convolution fusion | flops 75593728 | bytes 812160 | tf_op jit(solution)/shard_map/dot_general | solution.py:307
  6.8 1.7 %fusion.4 = f32[4,2,24,32]{3,2,1,0:T(8,128)S(1)} fusion(f32[4,2,24,8,128]{4,3,2,1,0:T(8,128)} %dn_ref.1, f32[8,32]{1,0:T(8,128)S(1)} %fusion.41, s32[32]{0:T(128)S(1)} %get-tuple-element.51), kind=kOutput, calls=%fused_computation.7 | convolution fusion | flops 75593728 | bytes 812160 | tf_op jit(solution)/shard_map/dot_general | solution.py:307
  8.6 0.4 copy.38
  9.0 0.6 gather_fusion
  10.0 0.8 %broadcast_in_dim.43 = f32[128,1,352]{2,1,0:T(1,128)} broadcast(f32[352]{0:T(512)S(1)} %broadcast_in_dim.42), dimensions={2} | broadcast | bytes 181632 | tf_op jit(solution)/shard_map/broadcast_in_dim | solution.py:22
  10.8 10.5 %all-to-all-start = ((f32[128,1,352]{2,1,0:T(1,128)}), f32[128,1,352]{2,1,0:T(1,128)S(1)}, u32[]{:S(2)}, u32[]{:S(2)}) async-start(f32[128,1,352]{2,1,0:T(1,128)} %broadcast_in_dim.43), calls=%async_computation | async-start | bytes 393216 | tf_op jit(solution)/shard_map/all_to_all | solution.py:23
  21.4 4.9 %shard_map.202 = (f32[24,8,20]{2,1,0:T(8,128)}, f32[24,8,18]{2,1,0:T(8,128)}, f32[24,20,128]{2,1,0:T(8,128)}, f32[24,18,128]{2,1,0:T(8,128)}) custom-call(f32[24,8,128]{2,1,0:T(8,128)} %pn_ref.1, f32[24,8,128]{2,1,0:T(8,128)} %sn_ref.1, f32[4,2,24,8,128]{4,3,2,1,0:T(8,128)} %dn_ref.1, f32[4,2,24,8,128]{4,3,2,1,0:T(8,128)} %wn_ref.1, f32[24,8,128]{2,1,0:T(8,128)} %tx_ref.3, ...), custom_call_target="tpu_custom_call" | custom-call | flops 3932160 | bytes 2162688 | tf_op jit(solution)/shard_map/pallas_call | solution.py:281
  26.3 3.1 %collective-permute-start = (f32[24,8,20]{2,1,0:T(8,128)}, f32[24,8,20]{2,1,0:T(8,128)S(1)}, u32[]{:S(2)}, u32[]{:S(2)}) collective-permute-start(f32[24,8,20]{2,1,0:T(8,128)} %get-tuple-element.10), channel_id=1, source_target_pairs={{0,32},{32,64},{64,96},{1,33},{33,65},{65,97},{2,34},{34,66},{66,9... | collective-permute-start | bytes 46088 | tf_op jit(solution)/shard_map/ppermute | solution.py:31
  29.4 2.2 %collective-permute-start.1 = (f32[24,8,18]{2,1,0:T(8,128)}, f32[24,8,18]{2,1,0:T(8,128)S(1)}, u32[]{:S(2)}, u32[]{:S(2)}) collective-permute-start(f32[24,8,18]{2,1,0:T(8,128)} %get-tuple-element.11), channel_id=1, source_target_pairs={{32,0},{64,32},{96,64},{33,1},{65,33},{97,65},{34,2},{66,34},{98,6... | collective-permute-start | bytes 41480 | tf_op jit(solution)/shard_map/ppermute | solution.py:31
  31.6 4.0 %collective-permute-start.2 = (f32[24,20,128]{2,1,0:T(8,128)}, f32[24,20,128]{2,1,0:T(8,128)S(1)}, u32[]{:S(2)}, u32[]{:S(2)}) collective-permute-start(f32[24,20,128]{2,1,0:T(8,128)} %get-tuple-element.12), channel_id=1, source_target_pairs={{0,1},{1,2},{2,3},{3,4},{4,5},{5,6},{6,7},{7,8},{8,9},{9,10},{10,1... | collective-permute-start | bytes 737288 | tf_op jit(solution)/shard_map/ppermute | solution.py:31
  35.6 1.9 %collective-permute-start.3 = (f32[24,18,128]{2,1,0:T(8,128)}, f32[24,18,128]{2,1,0:T(8,128)S(1)}, u32[]{:S(2)}, u32[]{:S(2)}) collective-permute-start(f32[24,18,128]{2,1,0:T(8,128)} %get-tuple-element.13), channel_id=1, source_target_pairs={{1,0},{2,1},{3,2},{4,3},{5,4},{6,5},{7,6},{8,7},{9,8},{10,9},{11,1... | collective-permute-start | bytes 663560 | tf_op jit(solution)/shard_map/ppermute | solution.py:31
  38.4 0.4 fusion.14
  39.0 1.0 %fusion = f32[9,2,24,8,128]{4,3,2,1,0:T(8,128)S(1)} fusion(f32[8,32]{1,0:T(8,128)S(1)} %fusion.41, f32[9,2,24,32]{3,2,1,0:T(8,128)S(1)} %maximum_maximum_fusion, s32[32]{0:T(128)S(1)} %get-tuple-element.51), kind=kOutput, calls=%fused_computation.1 | convolution fusion | flops 169984000 | bytes 1825920 | tf_op jit(solution)/shard_map/dot_general | solution.py:355
  40.1 5.8 %collective-permute-done.3.hyu_ref = f32[24,18,128]{2,1,0:T(8,128)S(1)} collective-permute-done((f32[24,18,128]{2,1,0:T(8,128)}, f32[24,18,128]{2,1,0:T(8,128)S(1)}, u32[]{:S(2)}, u32[]{:S(2)}) %collective-permute-start.3) | collective-permute-done | bytes 221216 | tf_op jit(solution)/shard_map/ppermute | solution.py:31
  46.0 0.7 %copy-done.1 = f32[24,18,128]{2,1,0:T(8,128)} copy-done((f32[24,18,128]{2,1,0:T(8,128)}, f32[24,18,128]{2,1,0:T(8,128)S(1)}, u32[]{:S(2)}) %copy-start.1) | copy-done | bytes 221208
  46.7 0.7 %copy-done = f32[24,20,128]{2,1,0:T(8,128)} copy-done((f32[24,20,128]{2,1,0:T(8,128)}, f32[24,20,128]{2,1,0:T(8,128)S(1)}, u32[]{:S(2)}) %copy-start) | copy-done | bytes 245784
  47.4 7.1 %shard_map.203 = (f32[2,24,8,128]{3,2,1,0:T(8,128)}, f32[4,2,24,8,128]{4,3,2,1,0:T(8,128)}, f32[4,2,24,8,128]{4,3,2,1,0:T(8,128)}) custom-call(f32[24,8,128]{2,1,0:T(8,128)} %pn_ref.1, f32[24,8,128]{2,1,0:T(8,128)} %sn_ref.1, f32[24,8,128]{2,1,0:T(8,128)} %so_ref.1, f32[24,8,128]{2,1,0:T(8,128)} %pore_ref.1, f32[24,8,128]{2,1,0:T(8,128)} %tx_ref.3, ...), custom_call_target="tpu_custom_call" | custom-call | flops 29491200 | bytes 9043968 | tf_op jit(solution)/shard_map/pallas_call | solution.py:372
  54.5 1.6 %fusion.18 = f32[2,24,8,128]{3,2,1,0:T(8,128)} fusion(f32[2,24,8,128]{3,2,1,0:T(8,128)} %get-tuple-element.14, f32[9,2,24,8,128]{4,3,2,1,0:T(8,128)S(1)} %fusion), kind=kLoop, calls=%fused_computation.27 | loop fusion | flops 49152 | bytes 589824 | tf_op jit(solution)/shard_map/add | solution.py:421
  56.1 2.7 %slice_add_fusion = (f32[4,2,24,8,128]{4,3,2,1,0:T(8,128)}, f32[4,2,24,8,128]{4,3,2,1,0:T(8,128)}) fusion(f32[4,2,24,8,128]{4,3,2,1,0:T(8,128)} %get-tuple-element.16, f32[9,2,24,8,128]{4,3,2,1,0:T(8,128)S(1)} %fusion, f32[4,2,24,8,128]{4,3,2,1,0:T(8,128)} %get-tuple-element.15), kind=kLoop, calls=%fused_computation.17 | loop fusion | flops 393216 | bytes 4718592 | tf_op jit(solution)/shard_map/add | solution.py:423
  (52 shorter events, 1.5 us)
Async XLA Ops:
  0.6 7.9 %copy-start.4 = (f32[2048]{0:T(1024)S(1)}, f32[2048]{0:T(1024)}, u32[]{:S(2)}) copy-start(f32[2048]{0:T(1024)} %param.37) | copy-start | bytes 24580
  0.6 7.9 %copy-start.5 = (f32[2048]{0:T(1024)S(1)}, f32[2048]{0:T(1024)}, u32[]{:S(2)}) copy-start(f32[2048]{0:T(1024)} %param.36) | copy-start | bytes 24580
  0.7 9.0 %copy-start.7 = (s32[32]{0:T(128)S(1)}, s32[32]{0:T(128)}, u32[]{:S(2)}) copy-start(s32[32]{0:T(128)} %param.33) | copy-start | bytes 388
  0.7 9.0 %copy-start.8 = (s32[32]{0:T(128)S(1)}, s32[32]{0:T(128)}, u32[]{:S(2)}) copy-start(s32[32]{0:T(128)} %param.34) | copy-start | bytes 388
  0.7 9.0 %copy-start.6 = (f32[32]{0:T(128)S(1)}, f32[32]{0:T(128)}, u32[]{:S(2)}) copy-start(f32[32]{0:T(128)} %param.35) | copy-start | bytes 388
  10.8 26.7 %all-to-all-start = ((f32[128,1,352]{2,1,0:T(1,128)}), f32[128,1,352]{2,1,0:T(1,128)S(1)}, u32[]{:S(2)}, u32[]{:S(2)}) async-start(f32[128,1,352]{2,1,0:T(1,128)} %broadcast_in_dim.43), calls=%async_computation | async-start | bytes 393216 | tf_op jit(solution)/shard_map/all_to_all | solution.py:23
  26.3 13.8 %collective-permute-start = (f32[24,8,20]{2,1,0:T(8,128)}, f32[24,8,20]{2,1,0:T(8,128)S(1)}, u32[]{:S(2)}, u32[]{:S(2)}) collective-permute-start(f32[24,8,20]{2,1,0:T(8,128)} %get-tuple-element.10), channel_id=1, source_target_pairs={{0,32},{32,64},{64,96},{1,33},{33,65},{65,97},{2,34},{34,66},{66,9... | collective-permute-start | bytes 46088 | tf_op jit(solution)/shard_map/ppermute | solution.py:31
  29.4 10.7 %collective-permute-start.1 = (f32[24,8,18]{2,1,0:T(8,128)}, f32[24,8,18]{2,1,0:T(8,128)S(1)}, u32[]{:S(2)}, u32[]{:S(2)}) collective-permute-start(f32[24,8,18]{2,1,0:T(8,128)} %get-tuple-element.11), channel_id=1, source_target_pairs={{32,0},{64,32},{96,64},{33,1},{65,33},{97,65},{34,2},{66,34},{98,6... | collective-permute-start | bytes 41480 | tf_op jit(solution)/shard_map/ppermute | solution.py:31
  31.6 14.4 %collective-permute-start.2 = (f32[24,20,128]{2,1,0:T(8,128)}, f32[24,20,128]{2,1,0:T(8,128)S(1)}, u32[]{:S(2)}, u32[]{:S(2)}) collective-permute-start(f32[24,20,128]{2,1,0:T(8,128)} %get-tuple-element.12), channel_id=1, source_target_pairs={{0,1},{1,2},{2,3},{3,4},{4,5},{5,6},{6,7},{7,8},{8,9},{9,10},{10,1... | collective-permute-start | bytes 737288 | tf_op jit(solution)/shard_map/ppermute | solution.py:31
  35.6 10.4 %collective-permute-start.3 = (f32[24,18,128]{2,1,0:T(8,128)}, f32[24,18,128]{2,1,0:T(8,128)S(1)}, u32[]{:S(2)}, u32[]{:S(2)}) collective-permute-start(f32[24,18,128]{2,1,0:T(8,128)} %get-tuple-element.13), channel_id=1, source_target_pairs={{1,0},{2,1},{3,2},{4,3},{5,4},{6,5},{7,6},{8,7},{9,8},{10,9},{11,1... | collective-permute-start | bytes 663560 | tf_op jit(solution)/shard_map/ppermute | solution.py:31
  40.1 5.9 %copy-start.3 = (f32[24,8,18]{2,1,0:T(8,128)}, f32[24,8,18]{2,1,0:T(8,128)S(1)}, u32[]{:S(2)}) copy-start(f32[24,8,18]{2,1,0:T(8,128)S(1)} %collective-permute-done.1.hxr_ref) | copy-start | bytes 41476
  40.1 5.9 %copy-start.2 = (f32[24,8,20]{2,1,0:T(8,128)}, f32[24,8,20]{2,1,0:T(8,128)S(1)}, u32[]{:S(2)}) copy-start(f32[24,8,20]{2,1,0:T(8,128)S(1)} %collective-permute-done.hxl_ref) | copy-start | bytes 46084
  46.0 0.7 %copy-start.1 = (f32[24,18,128]{2,1,0:T(8,128)}, f32[24,18,128]{2,1,0:T(8,128)S(1)}, u32[]{:S(2)}) copy-start(f32[24,18,128]{2,1,0:T(8,128)S(1)} %collective-permute-done.3.hyu_ref) | copy-start | bytes 663556
  46.7 0.7 %copy-start = (f32[24,20,128]{2,1,0:T(8,128)}, f32[24,20,128]{2,1,0:T(8,128)S(1)}, u32[]{:S(2)}) copy-start(f32[24,20,128]{2,1,0:T(8,128)S(1)} %collective-permute-done.2.hyd_ref) | copy-start | bytes 737284

commit v2 on v0

--- a/solution.py
+++ b/solution.py
@@ -278,16 +278,28 @@
 
     nf = 2 + 4 * ndir
     vmem = pl.BlockSpec(memory_space=pltpu.VMEM)
+    pack_span = 6 if layers % 6 == 0 else layers
+
+    def pack_block(*lead, mid=rows, last=cols):
+        return pl.BlockSpec(tuple(lead) + (pack_span, mid, last), lambda b: (0,) * len(lead) + (b, 0, 0))
+
     x_low, x_high, y_low, y_high = pl.pallas_call(
         pack_kernel,
+        grid=(layers // pack_span,),
         out_shape=[
             jax.ShapeDtypeStruct((layers, rows, nf + 2), jnp.float32),
             jax.ShapeDtypeStruct((layers, rows, nf), jnp.float32),
             jax.ShapeDtypeStruct((layers, nf + 2, cols), jnp.float32),
             jax.ShapeDtypeStruct((layers, nf, cols), jnp.float32),
         ],
-        in_specs=[vmem] * 8,
-        out_specs=[vmem] * 4,
+        in_specs=[pack_block(), pack_block(), pack_block(ndir, 2), pack_block(ndir, 2)] + [pack_block()] * 4,
+        out_specs=[
+            pack_block(last=nf + 2),
+            pack_block(last=nf),
+            pack_block(mid=nf + 2),
+            pack_block(mid=nf),
+        ],
+        compiler_params=pltpu.CompilerParams(dimension_semantics=("arbitrary",)),
         cost_estimate=pl.CostEstimate(
             flops=layers * rows * cols * 160,
             transcendentals=0,

time: 55.5 us -> 55.6 us (level)
  no operation moved by 1% of the time
where the time goes in v2:
time: 55.6 us; the launch traced here: 55.1 us
  starting transfers between devices  21.7 us (39%)
  Pallas kernels  12.1 us (22%)
  other arithmetic  6.82 us (12%)
  waiting for transfers between devices  5.63 us (10%)
  local copies, waits for them, and re-layouts  4.41 us (8%)
  matrix products  3.34 us (6%)
  between operations  1.11 us (2%)
    ppermute x4, starting transfers between devices, shift_along(): return lax.ppermute(block, axis, pairs)  11.2 us
    all_to_all x1, starting transfers between devices, gather_everywhere(): lax.all_to_all(flat, GX_GY_WA, 0, 0, tiled=True)  10.5 us
    pallas_call x1, Pallas kernels, layer_body(): pl.pallas_call(stencil_kernel, grid=(blocks,), out_shape=[jax.ShapeDtypeS...  7.14 us
    ppermute x4, waiting for transfers between devices, shift_along(): return lax.ppermute(block, axis, pairs)  5.63 us
    pallas_call x1, Pallas kernels, layer_body(): pl.pallas_call(pack_kernel, grid=(layers // pack_span,), out_shape=[jax.S...  4.97 us
    add x1, other arithmetic, layer_body(): adjoint_products = adjoint_products + spread[1 + ndir:]  2.67 us
    dot_general x4, matrix products, at_perfs(): by_lane = jnp.dot(field, lane_hit, precision=lax.Precision.HIGHEST)  1.89 us
    add x1, other arithmetic, layer_body(): reduced_residual = reduced_residual + spread[0]  1.63 us
  transfers between devices with their start and end apart: 5, of which 1 were waited for; matrix products, arithmetic and copies ran while one was open for 4% of the time, Pallas kernels for 0%

profile of v2, /device:TPU:27, one launch (start us, length us, event | category | flops | bytes accessed | tf_op | source)
XLA Modules:
  0.0 55.1 jit_solution(8216120157477326791)
XLA Ops:
  0.7 0.8 %compare_and_fusion = pred[32]{0:T(512)(128)(4,1)S(1)} fusion(s32[32]{0:T(128)} %param.31), kind=kLoop, calls=%fused_computation.70 | loop fusion | flops 192 | bytes 160 | tf_op jit(solution)/shard_map/jit(_take)/and | solution.py:333
  1.5 0.7 %fusion.44 = (f32[32]{0:T(128)S(1)}, f32[1,32]{1,0:T(1,128)S(1)}, s32[32]{0:T(128)S(1)}) fusion(s32[32]{0:T(128)} %param.31), kind=kLoop, calls=%fused_computation.91 | loop fusion | flops 128 | bytes 512 | tf_op jit(solution)/shard_map/convert_element_type | solution.py:352
  2.2 0.7 %and_select_fusion.1 = (s32[32]{0:T(128)S(1)}, s32[32]{0:T(128)S(1)}) fusion(s32[32]{0:T(128)} %param.32), kind=kLoop, calls=%fused_computation.72 | loop fusion | flops 608 | bytes 384 | tf_op jit(solution)/shard_map/jit(remainder)/select_n | solution.py:317
  2.9 5.0 %shard_map.202 = (f32[24,8,20]{2,1,0:T(8,128)}, f32[24,8,18]{2,1,0:T(8,128)}, f32[24,20,128]{2,1,0:T(8,128)}, f32[24,18,128]{2,1,0:T(8,128)}) custom-call(f32[24,8,128]{2,1,0:T(8,128)} %pn_ref, f32[24,8,128]{2,1,0:T(8,128)} %sn_ref, f32[4,2,24,8,128]{4,3,2,1,0:T(8,128)} %dn_ref, f32[4,2,24,8,128]{4,3,2,1,0:T(8,128)} %wn_ref, f32[24,8,128]{2,1,0:T(8,128)} %tx_ref.3, ...), custom_call_target="tpu_custom_call" | custom-call | flops 3932160 | bytes 2162688 | tf_op jit(solution)/shard_map/pallas_call | solution.py:286
  7.9 0.3 fusion.5
  8.5 0.7 %fusion.3 = f32[4,2,24,32]{3,2,1,0:T(8,128)S(1)} fusion(f32[4,2,24,8,128]{4,3,2,1,0:T(8,128)S(1)} %copy-done.1, f32[8,32]{1,0:T(8,128)S(1)} %fusion.33, s32[32]{0:T(128)S(1)} %get-tuple-element.67), kind=kOutput, calls=%fused_computation.6 | convolution fusion | flops 75593728 | bytes 812160 | tf_op jit(solution)/shard_map/dot_general | solution.py:321
  9.3 0.7 %fusion.2 = f32[4,2,24,32]{3,2,1,0:T(8,128)S(1)} fusion(f32[4,2,24,8,128]{4,3,2,1,0:T(8,128)S(1)} %copy-done, f32[8,32]{1,0:T(8,128)S(1)} %fusion.33, s32[32]{0:T(128)S(1)} %get-tuple-element.67), kind=kOutput, calls=%fused_computation.5 | convolution fusion | flops 75593728 | bytes 812160 | tf_op jit(solution)/shard_map/dot_general | solution.py:321
  10.0 0.4 copy.28
  10.4 0.6 %gather_fusion = f32[32,2]{1,0:T(8,128)S(1)} fusion(f32[2,2048]{0,1:T(8,128)S(1)} %copy.28, s32[1024]{0:T(1024)S(1)} %pad_clamp_fusion), kind=kCustom, calls=%fused_computation | custom fusion | bytes 640 | tf_op jit(solution)/shard_map/jit(_take)/gather | solution.py:333
  11.4 0.8 %broadcast_in_dim.43 = f32[128,1,352]{2,1,0:T(1,128)} broadcast(f32[352]{0:T(512)S(1)} %broadcast_in_dim.42), dimensions={2} | broadcast | bytes 181632 | tf_op jit(solution)/shard_map/broadcast_in_dim | solution.py:22
  12.2 10.5 %all-to-all-start = ((f32[128,1,352]{2,1,0:T(1,128)}), f32[128,1,352]{2,1,0:T(1,128)S(1)}, u32[]{:S(2)}, u32[]{:S(2)}) async-start(f32[128,1,352]{2,1,0:T(1,128)} %broadcast_in_dim.43), calls=%async_computation | async-start | bytes 393216 | tf_op jit(solution)/shard_map/all_to_all | solution.py:23
  22.8 3.1 %collective-permute-start = (f32[24,8,20]{2,1,0:T(8,128)S(1)}, f32[24,8,20]{2,1,0:T(8,128)S(1)}, u32[]{:S(2)}, u32[]{:S(2)}) collective-permute-start(f32[24,8,20]{2,1,0:T(8,128)S(1)} %copy-done.14), channel_id=1, source_target_pairs={{0,32},{32,64},{64,96},{1,33},{33,65},{65,97},{2,34},{34,66},{66,9... | collective-permute-start | bytes 46088 | tf_op jit(solution)/shard_map/ppermute | solution.py:31
  25.9 2.2 %collective-permute-start.1 = (f32[24,8,18]{2,1,0:T(8,128)S(1)}, f32[24,8,18]{2,1,0:T(8,128)S(1)}, u32[]{:S(2)}, u32[]{:S(2)}) collective-permute-start(f32[24,8,18]{2,1,0:T(8,128)S(1)} %copy-done.15), channel_id=1, source_target_pairs={{32,0},{64,32},{96,64},{33,1},{65,33},{97,65},{34,2},{66,34},{98,6... | collective-permute-start | bytes 41480 | tf_op jit(solution)/shard_map/ppermute | solution.py:31
  28.1 4.0 %collective-permute-start.2 = (f32[24,20,128]{2,1,0:T(8,128)S(1)}, f32[24,20,128]{2,1,0:T(8,128)S(1)}, u32[]{:S(2)}, u32[]{:S(2)}) collective-permute-start(f32[24,20,128]{2,1,0:T(8,128)S(1)} %copy-done.12), channel_id=1, source_target_pairs={{0,1},{1,2},{2,3},{3,4},{4,5},{5,6},{6,7},{7,8},{8,9},{9,10},{10,1... | collective-permute-start | bytes 737288 | tf_op jit(solution)/shard_map/ppermute | solution.py:31
  32.1 1.9 %collective-permute-start.3 = (f32[24,18,128]{2,1,0:T(8,128)S(1)}, f32[24,18,128]{2,1,0:T(8,128)S(1)}, u32[]{:S(2)}, u32[]{:S(2)}) collective-permute-start(f32[24,18,128]{2,1,0:T(8,128)S(1)} %copy-done.13), channel_id=1, source_target_pairs={{1,0},{2,1},{3,2},{4,3},{5,4},{6,5},{7,6},{8,7},{9,8},{10,9},{11,1... | collective-permute-start | bytes 663560 | tf_op jit(solution)/shard_map/ppermute | solution.py:31
  34.7 0.3 reshape.530
  35.0 0.4 fusion.8
  35.6 1.0 %fusion = f32[9,2,24,8,128]{4,3,2,1,0:T(8,128)S(1)} fusion(f32[8,32]{1,0:T(8,128)S(1)} %fusion.33, f32[9,2,24,32]{3,2,1,0:T(8,128)S(1)} %maximum_maximum_fusion, s32[32]{0:T(128)S(1)} %get-tuple-element.67), kind=kOutput, calls=%fused_computation.1 | convolution fusion | flops 169984000 | bytes 1825920 | tf_op jit(solution)/shard_map/dot_general | solution.py:369
  36.6 5.6 %collective-permute-done.3.hyu_ref = f32[24,18,128]{2,1,0:T(8,128)S(1)} collective-permute-done((f32[24,18,128]{2,1,0:T(8,128)S(1)}, f32[24,18,128]{2,1,0:T(8,128)S(1)}, u32[]{:S(2)}, u32[]{:S(2)}) %collective-permute-start.3) | collective-permute-done | bytes 221216 | tf_op jit(solution)/shard_map/ppermute | solution.py:31
  42.3 0.7 %copy-done.5 = f32[24,18,128]{2,1,0:T(8,128)} copy-done((f32[24,18,128]{2,1,0:T(8,128)}, f32[24,18,128]{2,1,0:T(8,128)S(1)}, u32[]{:S(2)}) %copy-start.5) | copy-done | bytes 221208
  43.0 0.7 %copy-done.4 = f32[24,20,128]{2,1,0:T(8,128)} copy-done((f32[24,20,128]{2,1,0:T(8,128)}, f32[24,20,128]{2,1,0:T(8,128)S(1)}, u32[]{:S(2)}) %copy-start.4) | copy-done | bytes 245784
  43.7 7.1 %shard_map.203 = (f32[2,24,8,128]{3,2,1,0:T(8,128)}, f32[4,2,24,8,128]{4,3,2,1,0:T(8,128)}, f32[4,2,24,8,128]{4,3,2,1,0:T(8,128)}) custom-call(f32[24,8,128]{2,1,0:T(8,128)} %pn_ref, f32[24,8,128]{2,1,0:T(8,128)} %sn_ref, f32[24,8,128]{2,1,0:T(8,128)} %so_ref.1, f32[24,8,128]{2,1,0:T(8,128)} %pore_ref.1, f32[24,8,128]{2,1,0:T(8,128)} %tx_ref.3, ...), custom_call_target="tpu_custom_call" | custom-call | flops 29491200 | bytes 9043968 | tf_op jit(solution)/shard_map/pallas_call | solution.py:386
  50.8 1.6 %fusion.12 = f32[2,24,8,128]{3,2,1,0:T(8,128)} fusion(f32[2,24,8,128]{3,2,1,0:T(8,128)} %get-tuple-element.30, f32[9,2,24,8,128]{4,3,2,1,0:T(8,128)S(1)} %fusion), kind=kLoop, calls=%fused_computation.21 | loop fusion | flops 49152 | bytes 589824 | tf_op jit(solution)/shard_map/add | solution.py:435
  52.5 2.7 %slice_add_fusion = (f32[4,2,24,8,128]{4,3,2,1,0:T(8,128)}, f32[4,2,24,8,128]{4,3,2,1,0:T(8,128)}) fusion(f32[4,2,24,8,128]{4,3,2,1,0:T(8,128)} %get-tuple-element.32, f32[9,2,24,8,128]{4,3,2,1,0:T(8,128)S(1)} %fusion, f32[4,2,24,8,128]{4,3,2,1,0:T(8,128)} %get-tuple-element.31), kind=kLoop, calls=%fused_computation.13 | loop fusion | flops 393216 | bytes 4718592 | tf_op jit(solution)/shard_map/add | solution.py:437
  (68 shorter events, 1.5 us)
Async XLA Ops:
  0.6 7.9 %copy-start.1 = (f32[4,2,24,8,128]{4,3,2,1,0:T(8,128)S(1)}, f32[4,2,24,8,128]{4,3,2,1,0:T(8,128)}, u32[]{:S(2)}) copy-start(f32[4,2,24,8,128]{4,3,2,1,0:T(8,128)} %wn_ref) | copy-start | bytes 2359300
  0.6 8.6 %copy-start = (f32[4,2,24,8,128]{4,3,2,1,0:T(8,128)S(1)}, f32[4,2,24,8,128]{4,3,2,1,0:T(8,128)}, u32[]{:S(2)}) copy-start(f32[4,2,24,8,128]{4,3,2,1,0:T(8,128)} %dn_ref) | copy-start | bytes 2359300
  0.7 7.6 %copy-start.3 = (f32[24,8,128]{2,1,0:T(8,128)S(1)}, f32[24,8,128]{2,1,0:T(8,128)}, u32[]{:S(2)}) copy-start(f32[24,8,128]{2,1,0:T(8,128)} %sn_ref) | copy-start | bytes 294916
  0.7 7.3 %copy-start.2 = (f32[24,8,128]{2,1,0:T(8,128)S(1)}, f32[24,8,128]{2,1,0:T(8,128)}, u32[]{:S(2)}) copy-start(f32[24,8,128]{2,1,0:T(8,128)} %pn_ref) | copy-start | bytes 294916
  2.9 7.0 %copy-start.8 = (f32[2048]{0:T(1024)S(1)}, f32[2048]{0:T(1024)}, u32[]{:S(2)}) copy-start(f32[2048]{0:T(1024)} %param.37) | copy-start | bytes 24580
  2.9 7.0 %copy-start.9 = (f32[2048]{0:T(1024)S(1)}, f32[2048]{0:T(1024)}, u32[]{:S(2)}) copy-start(f32[2048]{0:T(1024)} %param.36) | copy-start | bytes 24580
  7.9 3.1 %copy-start.11 = (s32[32]{0:T(128)S(1)}, s32[32]{0:T(128)}, u32[]{:S(2)}) copy-start(s32[32]{0:T(128)} %param.33) | copy-start | bytes 388
  7.9 3.1 %copy-start.16 = (s32[32]{0:T(128)S(1)}, s32[32]{0:T(128)}, u32[]{:S(2)}) copy-start(s32[32]{0:T(128)} %param.34) | copy-start | bytes 388
  7.9 3.1 %copy-start.10 = (f32[32]{0:T(128)S(1)}, f32[32]{0:T(128)}, u32[]{:S(2)}) copy-start(f32[32]{0:T(128)} %param.35) | copy-start | bytes 388
  9.2 13.6 %copy-start.14 = (f32[24,8,20]{2,1,0:T(8,128)S(1)}, f32[24,8,20]{2,1,0:T(8,128)}, u32[]{:S(2)}) copy-start(f32[24,8,20]{2,1,0:T(8,128)} %get-tuple-element.26) | copy-start | bytes 46084
  9.2 16.7 %copy-start.15 = (f32[24,8,18]{2,1,0:T(8,128)S(1)}, f32[24,8,18]{2,1,0:T(8,128)}, u32[]{:S(2)}) copy-start(f32[24,8,18]{2,1,0:T(8,128)} %get-tuple-element.27) | copy-start | bytes 41476
  9.2 18.9 %copy-start.12 = (f32[24,20,128]{2,1,0:T(8,128)S(1)}, f32[24,20,128]{2,1,0:T(8,128)}, u32[]{:S(2)}) copy-start(f32[24,20,128]{2,1,0:T(8,128)} %get-tuple-element.28) | copy-start | bytes 737284
  9.2 22.9 %copy-start.13 = (f32[24,18,128]{2,1,0:T(8,128)S(1)}, f32[24,18,128]{2,1,0:T(8,128)}, u32[]{:S(2)}) copy-start(f32[24,18,128]{2,1,0:T(8,128)} %get-tuple-element.29) | copy-start | bytes 663556
  12.2 21.8 %all-to-all-start = ((f32[128,1,352]{2,1,0:T(1,128)}), f32[128,1,352]{2,1,0:T(1,128)S(1)}, u32[]{:S(2)}, u32[]{:S(2)}) async-start(f32[128,1,352]{2,1,0:T(1,128)} %broadcast_in_dim.43), calls=%async_computation | async-start | bytes 393216 | tf_op jit(solution)/shard_map/all_to_all | solution.py:23
  22.8 13.8 %collective-permute-start = (f32[24,8,20]{2,1,0:T(8,128)S(1)}, f32[24,8,20]{2,1,0:T(8,128)S(1)}, u32[]{:S(2)}, u32[]{:S(2)}) collective-permute-start(f32[24,8,20]{2,1,0:T(8,128)S(1)} %copy-done.14), channel_id=1, source_target_pairs={{0,32},{32,64},{64,96},{1,33},{33,65},{65,97},{2,34},{34,66},{66,9... | collective-permute-start | bytes 46088 | tf_op jit(solution)/shard_map/ppermute | solution.py:31
  25.9 10.7 %collective-permute-start.1 = (f32[24,8,18]{2,1,0:T(8,128)S(1)}, f32[24,8,18]{2,1,0:T(8,128)S(1)}, u32[]{:S(2)}, u32[]{:S(2)}) collective-permute-start(f32[24,8,18]{2,1,0:T(8,128)S(1)} %copy-done.15), channel_id=1, source_target_pairs={{32,0},{64,32},{96,64},{33,1},{65,33},{97,65},{34,2},{66,34},{98,6... | collective-permute-start | bytes 41480 | tf_op jit(solution)/shard_map/ppermute | solution.py:31
  28.1 14.2 %collective-permute-start.2 = (f32[24,20,128]{2,1,0:T(8,128)S(1)}, f32[24,20,128]{2,1,0:T(8,128)S(1)}, u32[]{:S(2)}, u32[]{:S(2)}) collective-permute-start(f32[24,20,128]{2,1,0:T(8,128)S(1)} %copy-done.12), channel_id=1, source_target_pairs={{0,1},{1,2},{2,3},{3,4},{4,5},{5,6},{6,7},{7,8},{8,9},{9,10},{10,1... | collective-permute-start | bytes 737288 | tf_op jit(solution)/shard_map/ppermute | solution.py:31
  32.1 10.2 %collective-permute-start.3 = (f32[24,18,128]{2,1,0:T(8,128)S(1)}, f32[24,18,128]{2,1,0:T(8,128)S(1)}, u32[]{:S(2)}, u32[]{:S(2)}) collective-permute-start(f32[24,18,128]{2,1,0:T(8,128)S(1)} %copy-done.13), channel_id=1, source_target_pairs={{1,0},{2,1},{3,2},{4,3},{5,4},{6,5},{7,6},{8,7},{9,8},{10,9},{11,1... | collective-permute-start | bytes 663560 | tf_op jit(solution)/shard_map/ppermute | solution.py:31
  36.6 5.7 %copy-start.7 = (f32[24,8,18]{2,1,0:T(8,128)}, f32[24,8,18]{2,1,0:T(8,128)S(1)}, u32[]{:S(2)}) copy-start(f32[24,8,18]{2,1,0:T(8,128)S(1)} %collective-permute-done.1.hxr_ref) | copy-start | bytes 41476
  36.6 5.6 %copy-start.6 = (f32[24,8,20]{2,1,0:T(8,128)}, f32[24,8,20]{2,1,0:T(8,128)S(1)}, u32[]{:S(2)}) copy-start(f32[24,8,20]{2,1,0:T(8,128)S(1)} %collective-permute-done.hxl_ref) | copy-start | bytes 46084
  42.3 0.7 %copy-start.5 = (f32[24,18,128]{2,1,0:T(8,128)}, f32[24,18,128]{2,1,0:T(8,128)S(1)}, u32[]{:S(2)}) copy-start(f32[24,18,128]{2,1,0:T(8,128)S(1)} %collective-permute-done.3.hyu_ref) | copy-start | bytes 663556
  43.0 0.7 %copy-start.4 = (f32[24,20,128]{2,1,0:T(8,128)}, f32[24,20,128]{2,1,0:T(8,128)S(1)}, u32[]{:S(2)}) copy-start(f32[24,20,128]{2,1,0:T(8,128)S(1)} %collective-permute-done.2.hyd_ref) | copy-start | bytes 737284

commit v3 on v2

--- a/solution.py
+++ b/solution.py
@@ -83,13 +83,17 @@
     def rolled(x, shift, axis):
         return x if shift == 0 else pltpu.roll(x, shift, axis)
 
-    def rows_into(ref, k, tiles, source_row):
-        count = len(tiles)
+    def row_of(ref, lead, r):
+        v = ref[lead + (pl.ds(r, 1), slice(None))]
+        return jnp.broadcast_to(v.astype(jnp.float32), (rows, cols))
+
+    def rows_into(ref, k, sources, source_row):
+        count = len(sources)
         for start in range(0, count, rows):
             acc = jnp.zeros((rows, cols), jnp.float32)
             for f in range(start, min(start + rows, count)):
-                r = f - start
-                acc = jnp.where(sub == r, rolled(tiles[f], (r - source_row) % rows, 0), acc)
+                src, lead = sources[f]
+                acc = jnp.where(sub == f - start, row_of(src, lead, source_row), acc)
             n = min(rows, count - start)
             ref[k, pl.ds(start, n), :] = acc[:n]
 
@@ -99,8 +103,12 @@
             cells += [d_ref[d, half, k] for d in range(ndir)]
         for half in range(2):
             cells += [w_ref[d, half, k] for d in range(ndir)]
+        sources = [(p_ref, (k,)), (s_ref, (k,))]
+        for half in range(2):
+            sources += [(d_ref, (d, half, k)) for d in range(ndir)]
+        for half in range(2):
+            sources += [(w_ref, (d, half, k)) for d in range(ndir)]
         low_x = cells + [tx_ref[k], ux_ref[k].astype(jnp.float32)]
-        low_y = cells + [ty_ref[k], uy_ref[k].astype(jnp.float32)]
         xl = jnp.zeros((rows, cols), jnp.float32)
         for f, t in enumerate(low_x):
             xl = jnp.where(lane == f, rolled(t, (f - (cols - 1)) % cols, 1), xl)
@@ -109,8 +117,8 @@
             xr = jnp.where(lane == f, rolled(t, f % cols, 1), xr)
         xl_ref[k] = xl[:, : nf + 2]
         xr_ref[k] = xr[:, :nf]
-        rows_into(yd_ref, k, low_y, rows - 1)
-        rows_into(yu_ref, k, cells, 0)
+        rows_into(yd_ref, k, sources + [(ty_ref, (k,)), (uy_ref, (k,))], rows - 1)
+        rows_into(yu_ref, k, sources, 0)
         return carry
 
     lax.fori_loop(0, layers, body, 0)

time: 55.6 us -> 55.7 us (level)
  no operation moved by 1% of the time
where the time goes in v3:
time: 55.7 us; the launch traced here: 55.2 us
  starting transfers between devices  21.7 us (39%)
  Pallas kernels  12.1 us (22%)
  other arithmetic  6.82 us (12%)
  waiting for transfers between devices  5.63 us (10%)
  local copies, waits for them, and re-layouts  4.41 us (8%)
  matrix products  3.33 us (6%)
  between operations  1.11 us (2%)
    ppermute x4, starting transfers between devices, shift_along(): return lax.ppermute(block, axis, pairs)  11.2 us
    all_to_all x1, starting transfers between devices, gather_everywhere(): lax.all_to_all(flat, GX_GY_WA, 0, 0, tiled=True)  10.5 us
    pallas_call x1, Pallas kernels, layer_body(): pl.pallas_call(stencil_kernel, grid=(blocks,), out_shape=[jax.ShapeDtypeS...  7.14 us
    ppermute x4, waiting for transfers between devices, shift_along(): return lax.ppermute(block, axis, pairs)  5.63 us
    pallas_call x1, Pallas kernels, layer_body(): pl.pallas_call(pack_kernel, grid=(layers // pack_span,), out_shape=[jax.S...  5 us
    add x1, other arithmetic, layer_body(): adjoint_products = adjoint_products + spread[1 + ndir:]  2.67 us
    dot_general x4, matrix products, at_perfs(): by_lane = jnp.dot(field, lane_hit, precision=lax.Precision.HIGHEST)  1.88 us
    add x1, other arithmetic, layer_body(): reduced_residual = reduced_residual + spread[0]  1.63 us
  transfers between devices with their start and end apart: 5, of which 1 were waited for; matrix products, arithmetic and copies ran while one was open for 4% of the time, Pallas kernels for 0%

profile of v3, /device:TPU:27, one launch (start us, length us, event | category | flops | bytes accessed | tf_op | source)
XLA Modules:
  0.0 55.2 jit_solution(14941398190847445647)
XLA Ops:
  0.7 0.8 %compare_and_fusion = pred[32]{0:T(512)(128)(4,1)S(1)} fusion(s32[32]{0:T(128)} %param.31), kind=kLoop, calls=%fused_computation.70 | loop fusion | flops 192 | bytes 160 | tf_op jit(solution)/shard_map/jit(_take)/and | solution.py:341
  1.5 0.7 %fusion.44 = (f32[32]{0:T(128)S(1)}, f32[1,32]{1,0:T(1,128)S(1)}, s32[32]{0:T(128)S(1)}) fusion(s32[32]{0:T(128)} %param.31), kind=kLoop, calls=%fused_computation.91 | loop fusion | flops 128 | bytes 512 | tf_op jit(solution)/shard_map/convert_element_type | solution.py:360
  2.2 0.7 %and_select_fusion.1 = (s32[32]{0:T(128)S(1)}, s32[32]{0:T(128)S(1)}) fusion(s32[32]{0:T(128)} %param.32), kind=kLoop, calls=%fused_computation.72 | loop fusion | flops 608 | bytes 384 | tf_op jit(solution)/shard_map/jit(remainder)/select_n | solution.py:325
  2.9 5.0 %shard_map.202 = (f32[24,8,20]{2,1,0:T(8,128)}, f32[24,8,18]{2,1,0:T(8,128)}, f32[24,20,128]{2,1,0:T(8,128)}, f32[24,18,128]{2,1,0:T(8,128)}) custom-call(f32[24,8,128]{2,1,0:T(8,128)} %pn_ref, f32[24,8,128]{2,1,0:T(8,128)} %sn_ref, f32[4,2,24,8,128]{4,3,2,1,0:T(8,128)} %dn_ref, f32[4,2,24,8,128]{4,3,2,1,0:T(8,128)} %wn_ref, f32[24,8,128]{2,1,0:T(8,128)} %tx_ref.3, ...), custom_call_target="tpu_custom_call" | custom-call | flops 3932160 | bytes 2162688 | tf_op jit(solution)/shard_map/pallas_call | solution.py:294
  8.3 0.3 fusion.4
  8.5 0.7 %fusion.3 = f32[4,2,24,32]{3,2,1,0:T(8,128)S(1)} fusion(f32[4,2,24,8,128]{4,3,2,1,0:T(8,128)S(1)} %copy-done.1, f32[8,32]{1,0:T(8,128)S(1)} %fusion.33, s32[32]{0:T(128)S(1)} %get-tuple-element.67), kind=kOutput, calls=%fused_computation.6 | convolution fusion | flops 75593728 | bytes 812160 | tf_op jit(solution)/shard_map/dot_general | solution.py:329
  9.3 0.7 %fusion.2 = f32[4,2,24,32]{3,2,1,0:T(8,128)S(1)} fusion(f32[4,2,24,8,128]{4,3,2,1,0:T(8,128)S(1)} %copy-done, f32[8,32]{1,0:T(8,128)S(1)} %fusion.33, s32[32]{0:T(128)S(1)} %get-tuple-element.67), kind=kOutput, calls=%fused_computation.5 | convolution fusion | flops 75593728 | bytes 812160 | tf_op jit(solution)/shard_map/dot_general | solution.py:329
  10.0 0.4 copy.28
  10.4 0.6 %gather_fusion = f32[32,2]{1,0:T(8,128)S(1)} fusion(f32[2,2048]{0,1:T(8,128)S(1)} %copy.28, s32[1024]{0:T(1024)S(1)} %pad_clamp_fusion), kind=kCustom, calls=%fused_computation | custom fusion | bytes 640 | tf_op jit(solution)/shard_map/jit(_take)/gather | solution.py:341
  11.5 0.8 %broadcast_in_dim.43 = f32[128,1,352]{2,1,0:T(1,128)} broadcast(f32[352]{0:T(512)S(1)} %broadcast_in_dim.42), dimensions={2} | broadcast | bytes 181632 | tf_op jit(solution)/shard_map/broadcast_in_dim | solution.py:22
  12.3 10.5 %all-to-all-start = ((f32[128,1,352]{2,1,0:T(1,128)}), f32[128,1,352]{2,1,0:T(1,128)S(1)}, u32[]{:S(2)}, u32[]{:S(2)}) async-start(f32[128,1,352]{2,1,0:T(1,128)} %broadcast_in_dim.43), calls=%async_computation | async-start | bytes 393216 | tf_op jit(solution)/shard_map/all_to_all | solution.py:23
  22.8 3.1 %collective-permute-start = (f32[24,8,20]{2,1,0:T(8,128)S(1)}, f32[24,8,20]{2,1,0:T(8,128)S(1)}, u32[]{:S(2)}, u32[]{:S(2)}) collective-permute-start(f32[24,8,20]{2,1,0:T(8,128)S(1)} %copy-done.14), channel_id=1, source_target_pairs={{0,32},{32,64},{64,96},{1,33},{33,65},{65,97},{2,34},{34,66},{66,9... | collective-permute-start | bytes 46088 | tf_op jit(solution)/shard_map/ppermute | solution.py:31
  25.9 2.2 %collective-permute-start.1 = (f32[24,8,18]{2,1,0:T(8,128)S(1)}, f32[24,8,18]{2,1,0:T(8,128)S(1)}, u32[]{:S(2)}, u32[]{:S(2)}) collective-permute-start(f32[24,8,18]{2,1,0:T(8,128)S(1)} %copy-done.15), channel_id=1, source_target_pairs={{32,0},{64,32},{96,64},{33,1},{65,33},{97,65},{34,2},{66,34},{98,6... | collective-permute-start | bytes 41480 | tf_op jit(solution)/shard_map/ppermute | solution.py:31
  28.1 4.0 %collective-permute-start.2 = (f32[24,20,128]{2,1,0:T(8,128)S(1)}, f32[24,20,128]{2,1,0:T(8,128)S(1)}, u32[]{:S(2)}, u32[]{:S(2)}) collective-permute-start(f32[24,20,128]{2,1,0:T(8,128)S(1)} %copy-done.12), channel_id=1, source_target_pairs={{0,1},{1,2},{2,3},{3,4},{4,5},{5,6},{6,7},{7,8},{8,9},{9,10},{10,1... | collective-permute-start | bytes 737288 | tf_op jit(solution)/shard_map/ppermute | solution.py:31
  32.1 1.9 %collective-permute-start.3 = (f32[24,18,128]{2,1,0:T(8,128)S(1)}, f32[24,18,128]{2,1,0:T(8,128)S(1)}, u32[]{:S(2)}, u32[]{:S(2)}) collective-permute-start(f32[24,18,128]{2,1,0:T(8,128)S(1)} %copy-done.13), channel_id=1, source_target_pairs={{1,0},{2,1},{3,2},{4,3},{5,4},{6,5},{7,6},{8,7},{9,8},{10,9},{11,1... | collective-permute-start | bytes 663560 | tf_op jit(solution)/shard_map/ppermute | solution.py:31
  34.7 0.3 reshape.530
  35.0 0.4 fusion.8
  35.6 1.0 %fusion = f32[9,2,24,8,128]{4,3,2,1,0:T(8,128)S(1)} fusion(f32[8,32]{1,0:T(8,128)S(1)} %fusion.33, f32[9,2,24,32]{3,2,1,0:T(8,128)S(1)} %maximum_maximum_fusion, s32[32]{0:T(128)S(1)} %get-tuple-element.67), kind=kOutput, calls=%fused_computation.1 | convolution fusion | flops 169984000 | bytes 1825920 | tf_op jit(solution)/shard_map/dot_general | solution.py:377
  36.7 5.6 %collective-permute-done.3.hyu_ref = f32[24,18,128]{2,1,0:T(8,128)S(1)} collective-permute-done((f32[24,18,128]{2,1,0:T(8,128)S(1)}, f32[24,18,128]{2,1,0:T(8,128)S(1)}, u32[]{:S(2)}, u32[]{:S(2)}) %collective-permute-start.3) | collective-permute-done | bytes 221216 | tf_op jit(solution)/shard_map/ppermute | solution.py:31
  42.3 0.7 %copy-done.5 = f32[24,18,128]{2,1,0:T(8,128)} copy-done((f32[24,18,128]{2,1,0:T(8,128)}, f32[24,18,128]{2,1,0:T(8,128)S(1)}, u32[]{:S(2)}) %copy-start.5) | copy-done | bytes 221208
  43.0 0.7 %copy-done.4 = f32[24,20,128]{2,1,0:T(8,128)} copy-done((f32[24,20,128]{2,1,0:T(8,128)}, f32[24,20,128]{2,1,0:T(8,128)S(1)}, u32[]{:S(2)}) %copy-start.4) | copy-done | bytes 245784
  43.7 7.1 %shard_map.203 = (f32[2,24,8,128]{3,2,1,0:T(8,128)}, f32[4,2,24,8,128]{4,3,2,1,0:T(8,128)}, f32[4,2,24,8,128]{4,3,2,1,0:T(8,128)}) custom-call(f32[24,8,128]{2,1,0:T(8,128)} %pn_ref, f32[24,8,128]{2,1,0:T(8,128)} %sn_ref, f32[24,8,128]{2,1,0:T(8,128)} %so_ref.1, f32[24,8,128]{2,1,0:T(8,128)} %pore_ref.1, f32[24,8,128]{2,1,0:T(8,128)} %tx_ref.3, ...), custom_call_target="tpu_custom_call" | custom-call | flops 29491200 | bytes 9043968 | tf_op jit(solution)/shard_map/pallas_call | solution.py:394
  50.9 1.6 %fusion.12 = f32[2,24,8,128]{3,2,1,0:T(8,128)} fusion(f32[2,24,8,128]{3,2,1,0:T(8,128)} %get-tuple-element.30, f32[9,2,24,8,128]{4,3,2,1,0:T(8,128)S(1)} %fusion), kind=kLoop, calls=%fused_computation.21 | loop fusion | flops 49152 | bytes 589824 | tf_op jit(solution)/shard_map/add | solution.py:443
  52.5 2.7 %slice_add_fusion = (f32[4,2,24,8,128]{4,3,2,1,0:T(8,128)}, f32[4,2,24,8,128]{4,3,2,1,0:T(8,128)}) fusion(f32[4,2,24,8,128]{4,3,2,1,0:T(8,128)} %get-tuple-element.32, f32[9,2,24,8,128]{4,3,2,1,0:T(8,128)S(1)} %fusion, f32[4,2,24,8,128]{4,3,2,1,0:T(8,128)} %get-tuple-element.31), kind=kLoop, calls=%fused_computation.13 | loop fusion | flops 393216 | bytes 4718592 | tf_op jit(solution)/shard_map/add | solution.py:445
  (68 shorter events, 1.5 us)
Async XLA Ops:
  0.6 7.9 %copy-start.1 = (f32[4,2,24,8,128]{4,3,2,1,0:T(8,128)S(1)}, f32[4,2,24,8,128]{4,3,2,1,0:T(8,128)}, u32[]{:S(2)}) copy-start(f32[4,2,24,8,128]{4,3,2,1,0:T(8,128)} %wn_ref) | copy-start | bytes 2359300
  0.6 8.6 %copy-start = (f32[4,2,24,8,128]{4,3,2,1,0:T(8,128)S(1)}, f32[4,2,24,8,128]{4,3,2,1,0:T(8,128)}, u32[]{:S(2)}) copy-start(f32[4,2,24,8,128]{4,3,2,1,0:T(8,128)} %dn_ref) | copy-start | bytes 2359300
  0.7 7.6 %copy-start.3 = (f32[24,8,128]{2,1,0:T(8,128)S(1)}, f32[24,8,128]{2,1,0:T(8,128)}, u32[]{:S(2)}) copy-start(f32[24,8,128]{2,1,0:T(8,128)} %sn_ref) | copy-start | bytes 294916
  0.7 7.3 %copy-start.2 = (f32[24,8,128]{2,1,0:T(8,128)S(1)}, f32[24,8,128]{2,1,0:T(8,128)}, u32[]{:S(2)}) copy-start(f32[24,8,128]{2,1,0:T(8,128)} %pn_ref) | copy-start | bytes 294916
  2.9 7.1 %copy-start.8 = (f32[2048]{0:T(1024)S(1)}, f32[2048]{0:T(1024)}, u32[]{:S(2)}) copy-start(f32[2048]{0:T(1024)} %param.37) | copy-start | bytes 24580
  2.9 7.1 %copy-start.9 = (f32[2048]{0:T(1024)S(1)}, f32[2048]{0:T(1024)}, u32[]{:S(2)}) copy-start(f32[2048]{0:T(1024)} %param.36) | copy-start | bytes 24580
  7.9 3.1 %copy-start.11 = (s32[32]{0:T(128)S(1)}, s32[32]{0:T(128)}, u32[]{:S(2)}) copy-start(s32[32]{0:T(128)} %param.33) | copy-start | bytes 388
  7.9 3.1 %copy-start.16 = (s32[32]{0:T(128)S(1)}, s32[32]{0:T(128)}, u32[]{:S(2)}) copy-start(s32[32]{0:T(128)} %param.34) | copy-start | bytes 388
  8.0 3.1 %copy-start.10 = (f32[32]{0:T(128)S(1)}, f32[32]{0:T(128)}, u32[]{:S(2)}) copy-start(f32[32]{0:T(128)} %param.35) | copy-start | bytes 388
  9.2 13.6 %copy-start.14 = (f32[24,8,20]{2,1,0:T(8,128)S(1)}, f32[24,8,20]{2,1,0:T(8,128)}, u32[]{:S(2)}) copy-start(f32[24,8,20]{2,1,0:T(8,128)} %get-tuple-element.26) | copy-start | bytes 46084
  9.2 16.7 %copy-start.15 = (f32[24,8,18]{2,1,0:T(8,128)S(1)}, f32[24,8,18]{2,1,0:T(8,128)}, u32[]{:S(2)}) copy-start(f32[24,8,18]{2,1,0:T(8,128)} %get-tuple-element.27) | copy-start | bytes 41476
  9.3 18.9 %copy-start.12 = (f32[24,20,128]{2,1,0:T(8,128)S(1)}, f32[24,20,128]{2,1,0:T(8,128)}, u32[]{:S(2)}) copy-start(f32[24,20,128]{2,1,0:T(8,128)} %get-tuple-element.28) | copy-start | bytes 737284
  9.3 22.9 %copy-start.13 = (f32[24,18,128]{2,1,0:T(8,128)S(1)}, f32[24,18,128]{2,1,0:T(8,128)}, u32[]{:S(2)}) copy-start(f32[24,18,128]{2,1,0:T(8,128)} %get-tuple-element.29) | copy-start | bytes 663556
  12.3 21.8 %all-to-all-start = ((f32[128,1,352]{2,1,0:T(1,128)}), f32[128,1,352]{2,1,0:T(1,128)S(1)}, u32[]{:S(2)}, u32[]{:S(2)}) async-start(f32[128,1,352]{2,1,0:T(1,128)} %broadcast_in_dim.43), calls=%async_computation | async-start | bytes 393216 | tf_op jit(solution)/shard_map/all_to_all | solution.py:23
  22.8 13.8 %collective-permute-start = (f32[24,8,20]{2,1,0:T(8,128)S(1)}, f32[24,8,20]{2,1,0:T(8,128)S(1)}, u32[]{:S(2)}, u32[]{:S(2)}) collective-permute-start(f32[24,8,20]{2,1,0:T(8,128)S(1)} %copy-done.14), channel_id=1, source_target_pairs={{0,32},{32,64},{64,96},{1,33},{33,65},{65,97},{2,34},{34,66},{66,9... | collective-permute-start | bytes 46088 | tf_op jit(solution)/shard_map/ppermute | solution.py:31
  25.9 10.7 %collective-permute-start.1 = (f32[24,8,18]{2,1,0:T(8,128)S(1)}, f32[24,8,18]{2,1,0:T(8,128)S(1)}, u32[]{:S(2)}, u32[]{:S(2)}) collective-permute-start(f32[24,8,18]{2,1,0:T(8,128)S(1)} %copy-done.15), channel_id=1, source_target_pairs={{32,0},{64,32},{96,64},{33,1},{65,33},{97,65},{34,2},{66,34},{98,6... | collective-permute-start | bytes 41480 | tf_op jit(solution)/shard_map/ppermute | solution.py:31
  28.1 14.2 %collective-permute-start.2 = (f32[24,20,128]{2,1,0:T(8,128)S(1)}, f32[24,20,128]{2,1,0:T(8,128)S(1)}, u32[]{:S(2)}, u32[]{:S(2)}) collective-permute-start(f32[24,20,128]{2,1,0:T(8,128)S(1)} %copy-done.12), channel_id=1, source_target_pairs={{0,1},{1,2},{2,3},{3,4},{4,5},{5,6},{6,7},{7,8},{8,9},{9,10},{10,1... | collective-permute-start | bytes 737288 | tf_op jit(solution)/shard_map/ppermute | solution.py:31
  32.1 10.2 %collective-permute-start.3 = (f32[24,18,128]{2,1,0:T(8,128)S(1)}, f32[24,18,128]{2,1,0:T(8,128)S(1)}, u32[]{:S(2)}, u32[]{:S(2)}) collective-permute-start(f32[24,18,128]{2,1,0:T(8,128)S(1)} %copy-done.13), channel_id=1, source_target_pairs={{1,0},{2,1},{3,2},{4,3},{5,4},{6,5},{7,6},{8,7},{9,8},{10,9},{11,1... | collective-permute-start | bytes 663560 | tf_op jit(solution)/shard_map/ppermute | solution.py:31
  36.7 5.7 %copy-start.7 = (f32[24,8,18]{2,1,0:T(8,128)}, f32[24,8,18]{2,1,0:T(8,128)S(1)}, u32[]{:S(2)}) copy-start(f32[24,8,18]{2,1,0:T(8,128)S(1)} %collective-permute-done.1.hxr_ref) | copy-start | bytes 41476
  36.7 5.6 %copy-start.6 = (f32[24,8,20]{2,1,0:T(8,128)}, f32[24,8,20]{2,1,0:T(8,128)S(1)}, u32[]{:S(2)}) copy-start(f32[24,8,20]{2,1,0:T(8,128)S(1)} %collective-permute-done.hxl_ref) | copy-start | bytes 46084
  42.3 0.7 %copy-start.5 = (f32[24,18,128]{2,1,0:T(8,128)}, f32[24,18,128]{2,1,0:T(8,128)S(1)}, u32[]{:S(2)}) copy-start(f32[24,18,128]{2,1,0:T(8,128)S(1)} %collective-permute-done.3.hyu_ref) | copy-start | bytes 663556
  43.0 0.7 %copy-start.4 = (f32[24,20,128]{2,1,0:T(8,128)}, f32[24,20,128]{2,1,0:T(8,128)S(1)}, u32[]{:S(2)}) copy-start(f32[24,20,128]{2,1,0:T(8,128)S(1)} %collective-permute-done.2.hyd_ref) | copy-start | bytes 737284

commit v4 on v0

--- a/solution.py
+++ b/solution.py
@@ -341,10 +341,8 @@
     everyone = gather_everywhere(packed)
 
 
-    all_sums = jnp.moveaxis(everyone[:, :-1], 1, 0).reshape(row_sums.shape[0], -1)
-    all_wells = everyone[:, -1].reshape(-1)
-    same_well = (perf_well.astype(jnp.float32)[:, None] == all_wells[None, :]).astype(jnp.float32)
-    row_totals = jnp.dot(all_sums, same_well.T, precision=lax.Precision.HIGHEST)
+    same_well = (perf_well.astype(jnp.float32)[:, None, None] == everyone[None, :, -1, :]).astype(jnp.float32)
+    row_totals = jnp.einsum("dqc,rdc->qr", everyone[:, :-1], same_well, precision=lax.Precision.HIGHEST)
     row_factors = well_factors(row_totals, row_target)
     wells_res = rates - weight * mob * row_factors[0]
     wells_fwd = rate_tangent - (weight * mob)[None] * row_factors[1 : 1 + ndir][:, None, None, :]
@@ -420,9 +418,11 @@
         hyu,
     )
     reduced_residual, forward_products, adjoint_products = flux
-    reduced_residual = reduced_residual + spread[0]
-    forward_products = forward_products + spread[1 : 1 + ndir]
-    adjoint_products = adjoint_products + spread[1 + ndir :]
+    cell_row = perf_col // cols
+    cell_lane = perf_col % cols
+    reduced_residual = reduced_residual.at[..., cell_row, cell_lane].add(wells_res)
+    forward_products = forward_products.at[..., cell_row, cell_lane].add(wells_fwd)
+    adjoint_products = adjoint_products.at[..., cell_row, cell_lane].add(wells_adj)
     return (reduced_residual, forward_products, adjoint_products)
 
 

time: 55.5 us -> 81.9 us (1.48)
  local copies, waits for them, and re-layouts: 4.41 us -> 20.5 us
  other arithmetic: 6.82 us -> 12.3 us
  matrix products: 3.34 us -> 6.48 us
  waiting for transfers between devices: 5.63 us -> 6.95 us
    scatter-add x0 -> x3, other arithmetic: none -> 9.75 us  [the longest x1 3.85 us: layer_body(): adjoint_products.at[..., cell_row, cell_lane].add(wells_adj)]
    unnamed x34 -> x32, local copies, waits for them, and re-layouts: 1.5 us -> 9.65 us
    pallas_call x0 -> x3, local copies, waits for them, and re-layouts: none -> 7.59 us  [layer_body(): pl.pallas_call(stencil_kernel, grid=(blocks,), out_shape=[jax.ShapeDtypeS...]
    add x2 -> x0, other arithmetic: 4.3 us -> none  [the longest x1 2.67 us: layer_body(): adjoint_products = adjoint_products + spread[1 + ndir:]]
    dot_general x4, matrix products: 1.88 us -> 6.04 us  [at_perfs(): by_lane = jnp.dot(field, lane_hit, precision=lax.Precision.HIGHEST)]
    ppermute x4, waiting for transfers between devices: 5.63 us -> 6.94 us  [shift_along(): return lax.ppermute(block, axis, pairs)]
    dot_general x2 -> x1, matrix products: 1.45 us -> 0.44 us  [layer_body(): jnp.einsum('dqc,rdc->qr', everyone[:, :-1], same_well, precision=lax.Prec...]
  transfers between devices with their start and end apart: 5 -> 5, of which waited for: 1 -> 1; matrix products, arithmetic and copies ran while one was open for 4% -> 1% of each run, Pallas kernels for 0% -> 0%
where the time goes in v4:
time: 81.9 us; the launch traced here: 81.2 us
  starting transfers between devices  21.7 us (26%)
  local copies, waits for them, and re-layouts  20.5 us (25%)
  other arithmetic  12.3 us (15%)
  Pallas kernels  12.1 us (15%)
  waiting for transfers between devices  6.95 us (8%)
  matrix products  6.48 us (8%)
  between operations  1.08 us (1%)
    ppermute x4, starting transfers between devices, shift_along(): return lax.ppermute(block, axis, pairs)  11.2 us
    all_to_all x1, starting transfers between devices, gather_everywhere(): lax.all_to_all(flat, GX_GY_WA, 0, 0, tiled=True)  10.5 us
    unnamed x32, local copies, waits for them, and re-layouts  9.65 us
    pallas_call x3, local copies, waits for them, and re-layouts, layer_body(): pl.pallas_call(stencil_kernel, grid=(blocks,), out_shape=[jax.ShapeDtypeS...  7.59 us
    pallas_call x1, Pallas kernels, layer_body(): pl.pallas_call(stencil_kernel, grid=(blocks,), out_shape=[jax.ShapeDtypeS...  7.16 us
    ppermute x4, waiting for transfers between devices, shift_along(): return lax.ppermute(block, axis, pairs)  6.94 us
    dot_general x4, matrix products, at_perfs(): by_lane = jnp.dot(field, lane_hit, precision=lax.Precision.HIGHEST)  6.04 us
    pallas_call x1, Pallas kernels, layer_body(): pl.pallas_call(pack_kernel, out_shape=[jax.ShapeDtypeStruct((layers, rows...  4.93 us
  transfers between devices with their start and end apart: 5, of which 1 were waited for; matrix products, arithmetic and copies ran while one was open for 1% of the time, Pallas kernels for 0%

profile of v4, /device:TPU:27, one launch (start us, length us, event | category | flops | bytes accessed | tf_op | source)
XLA Modules:
  0.0 81.2 jit_solution(14356665227506725163)
XLA Ops:
  1.4 0.7 fusion.39
  2.9 4.9 %shard_map.202 = (f32[24,8,20]{2,1,0:T(8,128)}, f32[24,8,18]{2,1,0:T(8,128)}, f32[24,20,128]{2,1,0:T(8,128)}, f32[24,18,128]{2,1,0:T(8,128)}) custom-call(f32[24,8,128]{2,1,0:T(8,128)} %pn_ref, f32[24,8,128]{2,1,0:T(8,128)} %sn_ref, f32[4,2,24,8,128]{4,3,2,1,0:T(8,128)} %dn_ref, f32[4,2,24,8,128]{4,3,2,1,0:T(8,128)} %wn_ref, f32[24,8,128]{2,1,0:T(8,128)} %tx_ref.3, ...), custom_call_target="tpu_custom_call" | custom-call | flops 3932160 | bytes 2162688 | tf_op jit(solution)/shard_map/pallas_call | solution.py:281
  7.9 1.2 %fusion.3 = f32[24,32]{1,0:T(8,128)S(1)} fusion(f32[24,8,128]{2,1,0:T(8,128)} %pn_ref, f32[8,32]{1,0:T(8,128)S(1)} %fusion.26, s32[32]{0:T(128)S(1)} %get-tuple-element.53), kind=kOutput, calls=%fused_computation.11 | convolution fusion | flops 9452800 | bytes 102528 | tf_op jit(solution)/shard_map/dot_general | solution.py:309
  9.1 1.2 %fusion.2 = f32[24,32]{1,0:T(8,128)S(1)} fusion(f32[24,8,128]{2,1,0:T(8,128)} %sn_ref, f32[8,32]{1,0:T(8,128)S(1)} %fusion.26, s32[32]{0:T(128)S(1)} %get-tuple-element.53), kind=kOutput, calls=%fused_computation.10 | convolution fusion | flops 9452800 | bytes 102528 | tf_op jit(solution)/shard_map/dot_general | solution.py:309
  10.3 1.8 %fusion.1 = f32[4,2,24,32]{3,2,1,0:T(8,128)S(1)} fusion(f32[4,2,24,8,128]{4,3,2,1,0:T(8,128)} %wn_ref, f32[8,32]{1,0:T(8,128)S(1)} %fusion.26, s32[32]{0:T(128)S(1)} %get-tuple-element.53), kind=kOutput, calls=%fused_computation.7 | convolution fusion | flops 75593728 | bytes 812160 | tf_op jit(solution)/shard_map/dot_general | solution.py:309
  12.1 1.8 %fusion = f32[4,2,24,32]{3,2,1,0:T(8,128)S(1)} fusion(f32[4,2,24,8,128]{4,3,2,1,0:T(8,128)} %dn_ref, f32[8,32]{1,0:T(8,128)S(1)} %fusion.26, s32[32]{0:T(128)S(1)} %get-tuple-element.53), kind=kOutput, calls=%fused_computation.6 | convolution fusion | flops 75593728 | bytes 812160 | tf_op jit(solution)/shard_map/dot_general | solution.py:309
  16.3 0.8 broadcast_in_dim.49
  17.1 10.5 %all-to-all-start = ((f32[128,1,352]{2,1,0:T(1,128)}), f32[128,1,352]{2,1,0:T(1,128)S(1)}, u32[]{:S(2)}, u32[]{:S(2)}) async-start(f32[128,1,352]{2,1,0:T(1,128)} %broadcast_in_dim.49), calls=%async_computation | async-start | bytes 393216 | tf_op jit(solution)/shard_map/all_to_all | solution.py:23
  27.7 3.1 %collective-permute-start = (f32[24,8,20]{2,1,0:T(8,128)S(1)}, f32[24,8,20]{2,1,0:T(8,128)S(1)}, u32[]{:S(2)}, u32[]{:S(2)}) collective-permute-start(f32[24,8,20]{2,1,0:T(8,128)S(1)} %copy-done.11), channel_id=1, source_target_pairs={{0,32},{32,64},{64,96},{1,33},{33,65},{65,97},{2,34},{34,66},{66,9... | collective-permute-start | bytes 46088 | tf_op jit(solution)/shard_map/ppermute | solution.py:31
  30.8 2.2 %collective-permute-start.1 = (f32[24,8,18]{2,1,0:T(8,128)S(1)}, f32[24,8,18]{2,1,0:T(8,128)S(1)}, u32[]{:S(2)}, u32[]{:S(2)}) collective-permute-start(f32[24,8,18]{2,1,0:T(8,128)S(1)} %copy-done.12), channel_id=1, source_target_pairs={{32,0},{64,32},{96,64},{33,1},{65,33},{97,65},{34,2},{66,34},{98,6... | collective-permute-start | bytes 41480 | tf_op jit(solution)/shard_map/ppermute | solution.py:31
  33.0 4.0 %collective-permute-start.2 = (f32[24,20,128]{2,1,0:T(8,128)S(1)}, f32[24,20,128]{2,1,0:T(8,128)S(1)}, u32[]{:S(2)}, u32[]{:S(2)}) collective-permute-start(f32[24,20,128]{2,1,0:T(8,128)S(1)} %copy-done.9), channel_id=1, source_target_pairs={{0,1},{1,2},{2,3},{3,4},{4,5},{5,6},{6,7},{7,8},{8,9},{9,10},{10,1... | collective-permute-start | bytes 737288 | tf_op jit(solution)/shard_map/ppermute | solution.py:31
  37.0 1.9 %collective-permute-start.3 = (f32[24,18,128]{2,1,0:T(8,128)S(1)}, f32[24,18,128]{2,1,0:T(8,128)S(1)}, u32[]{:S(2)}, u32[]{:S(2)}) collective-permute-start(f32[24,18,128]{2,1,0:T(8,128)S(1)} %copy-done.10), channel_id=1, source_target_pairs={{1,0},{2,1},{3,2},{4,3},{5,4},{6,5},{7,6},{8,7},{9,8},{10,9},{11,1... | collective-permute-start | bytes 663560 | tf_op jit(solution)/shard_map/ppermute | solution.py:31
  40.2 6.9 %collective-permute-done.3.hyu_ref = f32[24,18,128]{2,1,0:T(8,128)S(1)} collective-permute-done((f32[24,18,128]{2,1,0:T(8,128)S(1)}, f32[24,18,128]{2,1,0:T(8,128)S(1)}, u32[]{:S(2)}, u32[]{:S(2)}) %collective-permute-start.3) | collective-permute-done | bytes 221216 | tf_op jit(solution)/shard_map/ppermute | solution.py:31
  47.8 0.7 copy-done.1
  48.6 7.2 %shard_map.203 = (f32[2,24,8,128]{3,2,1,0:T(8,128)}, f32[4,2,24,8,128]{4,3,2,1,0:T(8,128)}, f32[4,2,24,8,128]{4,3,2,1,0:T(8,128)}) custom-call(f32[24,8,128]{2,1,0:T(8,128)} %pn_ref, f32[24,8,128]{2,1,0:T(8,128)} %sn_ref, f32[24,8,128]{2,1,0:T(8,128)} %so_ref.1, f32[24,8,128]{2,1,0:T(8,128)} %pore_ref.1, f32[24,8,128]{2,1,0:T(8,128)} %tx_ref.3, ...), custom_call_target="tpu_custom_call" | custom-call | flops 29491200 | bytes 9043968 | tf_op jit(solution)/shard_map/pallas_call | solution.py:372
  55.7 1.4 %copy.86 = f32[2,24,8,128]{1,0,3,2:T(2,128)S(1)} copy(f32[2,24,8,128]{3,2,1,0:T(8,128)} %get-tuple-element.30) | data formatting | bytes 393216 | tf_op jit(solution)/shard_map/pallas_call | solution.py:372
  57.1 2.0 %scatter_fusion = f32[2,24,8,128]{1,0,3,2:T(2,128)S(1)} fusion(f32[2,24,8,128]{1,0,3,2:T(2,128)S(1)} %copy.86, s32[32]{0:T(128)S(1)} %get-tuple-element.51, f32[32,2,24]{2,1,0:T(2,128)S(1)} %copy.87), kind=kCustom, calls=%fused_computation.1 | custom fusion | flops 1536 | bytes 18688 | tf_op jit(solution)/shard_map/scatter-add | solution.py:423
  59.1 1.0 %copy.93 = f32[2,24,8,128]{3,2,1,0:T(8,128)} copy(f32[2,24,8,128]{1,0,3,2:T(2,128)S(1)} %scatter_fusion) | data formatting | bytes 393216
  60.2 3.6 %copy.90 = f32[4,2,24,8,128]{2,0,4,3,1:T(4,128)} copy(f32[4,2,24,8,128]{4,3,2,1,0:T(8,128)} %get-tuple-element.31) | data formatting | bytes 1572864 | tf_op jit(solution)/shard_map/pallas_call | solution.py:372
  63.8 3.9 %scatter_fusion.1 = f32[4,2,24,8,128]{2,0,4,3,1:T(4,128)} fusion(f32[4,2,24,8,128]{2,0,4,3,1:T(4,128)} %copy.90, s32[32]{0:T(128)S(1)} %get-tuple-element.51, f32[32,4,2,24]{3,1,2,0:T(4,128)S(1)} %subtract_bitcast_fusion), kind=kCustom, calls=%fused_computation.2 | custom fusion | flops 6144 | bytes 73984 | tf_op jit(solution)/shard_map/scatter-add | solution.py:424
  67.6 3.5 %copy.94 = f32[4,2,24,8,128]{4,3,2,1,0:T(8,128)} copy(f32[4,2,24,8,128]{2,0,4,3,1:T(4,128)} %scatter_fusion.1) | data formatting | bytes 1572864
  71.2 2.6 %copy.91 = f32[4,2,24,8,128]{2,0,4,3,1:T(4,128)} copy(f32[4,2,24,8,128]{4,3,2,1,0:T(8,128)S(1)} %copy-done) | data formatting | bytes 1572864 | tf_op jit(solution)/shard_map/pallas_call | solution.py:372
  73.8 3.9 %scatter_fusion.2 = f32[4,2,24,8,128]{2,0,4,3,1:T(4,128)} fusion(f32[4,2,24,8,128]{2,0,4,3,1:T(4,128)} %copy.91, s32[32]{0:T(128)S(1)} %get-tuple-element.51, f32[32,4,2,24]{3,1,2,0:T(4,128)S(1)} %copy.92), kind=kCustom, calls=%fused_computation.3 | custom fusion | flops 6144 | bytes 73984 | tf_op jit(solution)/shard_map/scatter-add | solution.py:425
  77.6 3.5 %copy.95 = f32[4,2,24,8,128]{4,3,2,1,0:T(8,128)} copy(f32[4,2,24,8,128]{2,0,4,3,1:T(4,128)} %scatter_fusion.2) | data formatting | bytes 1572864
  (78 shorter events, 5.6 us)
Async XLA Ops:
  0.6 13.5 %copy-start.5 = (f32[2048]{0:T(1024)S(1)}, f32[2048]{0:T(1024)}, u32[]{:S(2)}) copy-start(f32[2048]{0:T(1024)} %param.37) | copy-start | bytes 24580
  0.6 13.5 %copy-start.6 = (f32[2048]{0:T(1024)S(1)}, f32[2048]{0:T(1024)}, u32[]{:S(2)}) copy-start(f32[2048]{0:T(1024)} %param.36) | copy-start | bytes 24580
  0.7 14.6 %copy-start.8 = (s32[32]{0:T(128)S(1)}, s32[32]{0:T(128)}, u32[]{:S(2)}) copy-start(s32[32]{0:T(128)} %param.33) | copy-start | bytes 388
  0.7 14.6 %copy-start.13 = (s32[32]{0:T(128)S(1)}, s32[32]{0:T(128)}, u32[]{:S(2)}) copy-start(s32[32]{0:T(128)} %param.34) | copy-start | bytes 388
  0.7 14.6 %copy-start.7 = (f32[32]{0:T(128)S(1)}, f32[32]{0:T(128)}, u32[]{:S(2)}) copy-start(f32[32]{0:T(128)} %param.35) | copy-start | bytes 388
  7.8 19.8 %copy-start.11 = (f32[24,8,20]{2,1,0:T(8,128)S(1)}, f32[24,8,20]{2,1,0:T(8,128)}, u32[]{:S(2)}) copy-start(f32[24,8,20]{2,1,0:T(8,128)} %get-tuple-element.26) | copy-start | bytes 46084
  7.8 22.9 %copy-start.12 = (f32[24,8,18]{2,1,0:T(8,128)S(1)}, f32[24,8,18]{2,1,0:T(8,128)}, u32[]{:S(2)}) copy-start(f32[24,8,18]{2,1,0:T(8,128)} %get-tuple-element.27) | copy-start | bytes 41476
  7.8 25.1 %copy-start.9 = (f32[24,20,128]{2,1,0:T(8,128)S(1)}, f32[24,20,128]{2,1,0:T(8,128)}, u32[]{:S(2)}) copy-start(f32[24,20,128]{2,1,0:T(8,128)} %get-tuple-element.28) | copy-start | bytes 737284
  7.8 29.1 %copy-start.10 = (f32[24,18,128]{2,1,0:T(8,128)S(1)}, f32[24,18,128]{2,1,0:T(8,128)}, u32[]{:S(2)}) copy-start(f32[24,18,128]{2,1,0:T(8,128)} %get-tuple-element.29) | copy-start | bytes 663556
  17.1 21.9 %all-to-all-start = ((f32[128,1,352]{2,1,0:T(1,128)}), f32[128,1,352]{2,1,0:T(1,128)S(1)}, u32[]{:S(2)}, u32[]{:S(2)}) async-start(f32[128,1,352]{2,1,0:T(1,128)} %broadcast_in_dim.49), calls=%async_computation | async-start | bytes 393216 | tf_op jit(solution)/shard_map/all_to_all | solution.py:23
  27.7 12.5 %collective-permute-start = (f32[24,8,20]{2,1,0:T(8,128)S(1)}, f32[24,8,20]{2,1,0:T(8,128)S(1)}, u32[]{:S(2)}, u32[]{:S(2)}) collective-permute-start(f32[24,8,20]{2,1,0:T(8,128)S(1)} %copy-done.11), channel_id=1, source_target_pairs={{0,32},{32,64},{64,96},{1,33},{33,65},{65,97},{2,34},{34,66},{66,9... | collective-permute-start | bytes 46088 | tf_op jit(solution)/shard_map/ppermute | solution.py:31
  30.8 9.4 %collective-permute-start.1 = (f32[24,8,18]{2,1,0:T(8,128)S(1)}, f32[24,8,18]{2,1,0:T(8,128)S(1)}, u32[]{:S(2)}, u32[]{:S(2)}) collective-permute-start(f32[24,8,18]{2,1,0:T(8,128)S(1)} %copy-done.12), channel_id=1, source_target_pairs={{32,0},{64,32},{96,64},{33,1},{65,33},{97,65},{34,2},{66,34},{98,6... | collective-permute-start | bytes 41480 | tf_op jit(solution)/shard_map/ppermute | solution.py:31
  33.0 14.2 %collective-permute-start.2 = (f32[24,20,128]{2,1,0:T(8,128)S(1)}, f32[24,20,128]{2,1,0:T(8,128)S(1)}, u32[]{:S(2)}, u32[]{:S(2)}) collective-permute-start(f32[24,20,128]{2,1,0:T(8,128)S(1)} %copy-done.9), channel_id=1, source_target_pairs={{0,1},{1,2},{2,3},{3,4},{4,5},{5,6},{6,7},{7,8},{8,9},{9,10},{10,1... | collective-permute-start | bytes 737288 | tf_op jit(solution)/shard_map/ppermute | solution.py:31
  37.0 10.2 %collective-permute-start.3 = (f32[24,18,128]{2,1,0:T(8,128)S(1)}, f32[24,18,128]{2,1,0:T(8,128)S(1)}, u32[]{:S(2)}, u32[]{:S(2)}) collective-permute-start(f32[24,18,128]{2,1,0:T(8,128)S(1)} %copy-done.10), channel_id=1, source_target_pairs={{1,0},{2,1},{3,2},{4,3},{5,4},{6,5},{7,6},{8,7},{9,8},{10,9},{11,1... | collective-permute-start | bytes 663560 | tf_op jit(solution)/shard_map/ppermute | solution.py:31
  40.2 7.0 %copy-start.4 = (f32[24,8,18]{2,1,0:T(8,128)}, f32[24,8,18]{2,1,0:T(8,128)S(1)}, u32[]{:S(2)}) copy-start(f32[24,8,18]{2,1,0:T(8,128)S(1)} %collective-permute-done.1.hxr_ref) | copy-start | bytes 41476
  40.2 7.0 %copy-start.3 = (f32[24,8,20]{2,1,0:T(8,128)}, f32[24,8,20]{2,1,0:T(8,128)S(1)}, u32[]{:S(2)}) copy-start(f32[24,8,20]{2,1,0:T(8,128)S(1)} %collective-permute-done.hxl_ref) | copy-start | bytes 46084
  47.1 0.7 copy-start.2
  47.8 0.7 copy-start.1
  60.2 11.0 %copy-start = (f32[4,2,24,8,128]{4,3,2,1,0:T(8,128)S(1)}, f32[4,2,24,8,128]{4,3,2,1,0:T(8,128)}, u32[]{:S(2)}) copy-start(f32[4,2,24,8,128]{4,3,2,1,0:T(8,128)} %get-tuple-element.32) | copy-start | bytes 2359300

commit v5 on v0

--- a/solution.py
+++ b/solution.py
@@ -341,10 +341,8 @@
     everyone = gather_everywhere(packed)
 
 
-    all_sums = jnp.moveaxis(everyone[:, :-1], 1, 0).reshape(row_sums.shape[0], -1)
-    all_wells = everyone[:, -1].reshape(-1)
-    same_well = (perf_well.astype(jnp.float32)[:, None] == all_wells[None, :]).astype(jnp.float32)
-    row_totals = jnp.dot(all_sums, same_well.T, precision=lax.Precision.HIGHEST)
+    same_well = (perf_well.astype(jnp.float32)[:, None, None] == everyone[None, :, -1, :]).astype(jnp.float32)
+    row_totals = jnp.einsum("dqc,rdc->qr", everyone[:, :-1], same_well, precision=lax.Precision.HIGHEST)
     row_factors = well_factors(row_totals, row_target)
     wells_res = rates - weight * mob * row_factors[0]
     wells_fwd = rate_tangent - (weight * mob)[None] * row_factors[1 : 1 + ndir][:, None, None, :]
@@ -354,7 +352,7 @@
     )
     combined = jnp.concatenate([wells_res[None], wells_fwd, wells_adj], axis=0)
     by_row = combined[..., None, :] * row_hit
-    spread = jnp.dot(by_row, lane_hit.T, precision=lax.Precision.HIGHEST)
+    spread = jnp.dot(by_row, lane_hit.T, precision=lax.Precision.HIGH)
 
     span = 6 if layers % 6 == 0 else layers
     blocks = layers // span

time: 55.5 us -> 55.5 us (level)
  waiting for transfers between devices: 5.63 us -> 6.69 us
  local copies, waits for them, and re-layouts: 4.41 us -> 3.68 us
    ppermute x4, waiting for transfers between devices: 5.63 us -> 6.69 us  [shift_along(): return lax.ppermute(block, axis, pairs)]
  transfers between devices with their start and end apart: 5 -> 5, of which waited for: 1 -> 1; matrix products, arithmetic and copies ran while one was open for 4% -> 3% of each run, Pallas kernels for 0% -> 0%
where the time goes in v5:
time: 55.5 us; the launch traced here: 55.1 us
  starting transfers between devices  21.7 us (39%)
  Pallas kernels  12.1 us (22%)
  other arithmetic  6.82 us (12%)
  waiting for transfers between devices  6.69 us (12%)
  local copies, waits for them, and re-layouts  3.68 us (7%)
  matrix products  3.01 us (5%)
  between operations  1.09 us (2%)
    ppermute x4, starting transfers between devices, shift_along(): return lax.ppermute(block, axis, pairs)  11.2 us
    all_to_all x1, starting transfers between devices, gather_everywhere(): lax.all_to_all(flat, GX_GY_WA, 0, 0, tiled=True)  10.5 us
    pallas_call x1, Pallas kernels, layer_body(): pl.pallas_call(stencil_kernel, grid=(blocks,), out_shape=[jax.ShapeDtypeS...  7.14 us
    ppermute x4, waiting for transfers between devices, shift_along(): return lax.ppermute(block, axis, pairs)  6.69 us
    pallas_call x1, Pallas kernels, layer_body(): pl.pallas_call(pack_kernel, out_shape=[jax.ShapeDtypeStruct((layers, rows...  4.93 us
    add x1, other arithmetic, layer_body(): adjoint_products = adjoint_products + spread[1 + ndir:]  2.67 us
    dot_general x4, matrix products, at_perfs(): by_lane = jnp.dot(field, lane_hit, precision=lax.Precision.HIGHEST)  1.88 us
    add x1, other arithmetic, layer_body(): reduced_residual = reduced_residual + spread[0]  1.63 us
  transfers between devices with their start and end apart: 5, of which 1 were waited for; matrix products, arithmetic and copies ran while one was open for 3% of the time, Pallas kernels for 0%

profile of v5, /device:TPU:27, one launch (start us, length us, event | category | flops | bytes accessed | tf_op | source)
XLA Modules:
  0.0 55.1 jit_solution(1131718362900446312)
XLA Ops:
  0.7 0.8 %compare_and_fusion = pred[32]{0:T(512)(128)(4,1)S(1)} fusion(s32[32]{0:T(128)} %param.31), kind=kLoop, calls=%fused_computation.71 | loop fusion | flops 192 | bytes 160 | tf_op jit(solution)/shard_map/jit(_take)/and | solution.py:321
  1.5 0.7 %fusion.44 = (f32[32]{0:T(128)S(1)}, f32[1,32]{1,0:T(1,128)S(1)}, s32[32]{0:T(128)S(1)}) fusion(s32[32]{0:T(128)} %param.31), kind=kLoop, calls=%fused_computation.92 | loop fusion | flops 128 | bytes 512 | tf_op jit(solution)/shard_map/convert_element_type | solution.py:340
  2.2 0.7 %and_select_fusion.1 = (s32[32]{0:T(128)S(1)}, s32[32]{0:T(128)S(1)}) fusion(s32[32]{0:T(128)} %param.32), kind=kLoop, calls=%fused_computation.73 | loop fusion | flops 608 | bytes 384 | tf_op jit(solution)/shard_map/jit(remainder)/select_n | solution.py:305
  2.9 4.9 %shard_map.202 = (f32[24,8,20]{2,1,0:T(8,128)}, f32[24,8,18]{2,1,0:T(8,128)}, f32[24,20,128]{2,1,0:T(8,128)}, f32[24,18,128]{2,1,0:T(8,128)}) custom-call(f32[24,8,128]{2,1,0:T(8,128)} %pn_ref, f32[24,8,128]{2,1,0:T(8,128)} %sn_ref, f32[4,2,24,8,128]{4,3,2,1,0:T(8,128)} %dn_ref, f32[4,2,24,8,128]{4,3,2,1,0:T(8,128)} %wn_ref, f32[24,8,128]{2,1,0:T(8,128)} %tx_ref.3, ...), custom_call_target="tpu_custom_call" | custom-call | flops 3932160 | bytes 2162688 | tf_op jit(solution)/shard_map/pallas_call | solution.py:281
  7.9 0.3 fusion.5
  8.2 0.3 fusion.4
  8.5 0.7 %fusion.3 = f32[4,2,24,32]{3,2,1,0:T(8,128)S(1)} fusion(f32[4,2,24,8,128]{4,3,2,1,0:T(8,128)S(1)} %copy-done.1, f32[8,32]{1,0:T(8,128)S(1)} %fusion.33, s32[32]{0:T(128)S(1)} %get-tuple-element.67), kind=kOutput, calls=%fused_computation.6 | convolution fusion | flops 75593728 | bytes 812160 | tf_op jit(solution)/shard_map/dot_general | solution.py:309
  9.2 0.7 %fusion.2 = f32[4,2,24,32]{3,2,1,0:T(8,128)S(1)} fusion(f32[4,2,24,8,128]{4,3,2,1,0:T(8,128)S(1)} %copy-done, f32[8,32]{1,0:T(8,128)S(1)} %fusion.33, s32[32]{0:T(128)S(1)} %get-tuple-element.67), kind=kOutput, calls=%fused_computation.5 | convolution fusion | flops 75593728 | bytes 812160 | tf_op jit(solution)/shard_map/dot_general | solution.py:309
  9.9 0.4 copy.27
  10.3 0.6 %gather_fusion = f32[32,2]{1,0:T(8,128)S(1)} fusion(f32[2,2048]{0,1:T(8,128)S(1)} %copy.27, s32[1024]{0:T(1024)S(1)} %pad_clamp_fusion), kind=kCustom, calls=%fused_computation | custom fusion | bytes 640 | tf_op jit(solution)/shard_map/jit(_take)/gather | solution.py:321
  11.4 0.8 %broadcast_in_dim.43 = f32[128,1,352]{2,1,0:T(1,128)} broadcast(f32[352]{0:T(512)S(1)} %broadcast_in_dim.42), dimensions={2} | broadcast | bytes 181632 | tf_op jit(solution)/shard_map/broadcast_in_dim | solution.py:22
  12.2 10.5 %all-to-all-start = ((f32[128,1,352]{2,1,0:T(1,128)}), f32[128,1,352]{2,1,0:T(1,128)S(1)}, u32[]{:S(2)}, u32[]{:S(2)}) async-start(f32[128,1,352]{2,1,0:T(1,128)} %broadcast_in_dim.43), calls=%async_computation | async-start | bytes 393216 | tf_op jit(solution)/shard_map/all_to_all | solution.py:23
  22.7 3.1 %collective-permute-start = (f32[24,8,20]{2,1,0:T(8,128)S(1)}, f32[24,8,20]{2,1,0:T(8,128)S(1)}, u32[]{:S(2)}, u32[]{:S(2)}) collective-permute-start(f32[24,8,20]{2,1,0:T(8,128)S(1)} %copy-done.14), channel_id=1, source_target_pairs={{0,32},{32,64},{64,96},{1,33},{33,65},{65,97},{2,34},{34,66},{66,9... | collective-permute-start | bytes 46088 | tf_op jit(solution)/shard_map/ppermute | solution.py:31
  25.9 2.2 %collective-permute-start.1 = (f32[24,8,18]{2,1,0:T(8,128)S(1)}, f32[24,8,18]{2,1,0:T(8,128)S(1)}, u32[]{:S(2)}, u32[]{:S(2)}) collective-permute-start(f32[24,8,18]{2,1,0:T(8,128)S(1)} %copy-done.15), channel_id=1, source_target_pairs={{32,0},{64,32},{96,64},{33,1},{65,33},{97,65},{34,2},{66,34},{98,6... | collective-permute-start | bytes 41480 | tf_op jit(solution)/shard_map/ppermute | solution.py:31
  28.1 4.0 %collective-permute-start.2 = (f32[24,20,128]{2,1,0:T(8,128)S(1)}, f32[24,20,128]{2,1,0:T(8,128)S(1)}, u32[]{:S(2)}, u32[]{:S(2)}) collective-permute-start(f32[24,20,128]{2,1,0:T(8,128)S(1)} %copy-done.12), channel_id=1, source_target_pairs={{0,1},{1,2},{2,3},{3,4},{4,5},{5,6},{6,7},{7,8},{8,9},{9,10},{10,1... | collective-permute-start | bytes 737288 | tf_op jit(solution)/shard_map/ppermute | solution.py:31
  32.1 1.9 %collective-permute-start.3 = (f32[24,18,128]{2,1,0:T(8,128)S(1)}, f32[24,18,128]{2,1,0:T(8,128)S(1)}, u32[]{:S(2)}, u32[]{:S(2)}) collective-permute-start(f32[24,18,128]{2,1,0:T(8,128)S(1)} %copy-done.13), channel_id=1, source_target_pairs={{1,0},{2,1},{3,2},{4,3},{5,4},{6,5},{7,6},{8,7},{9,8},{10,9},{11,1... | collective-permute-start | bytes 663560 | tf_op jit(solution)/shard_map/ppermute | solution.py:31
  34.2 0.4 convolution_bitcast_fusion
  34.8 0.7 %fusion = f32[9,2,24,8,128]{4,3,2,1,0:T(8,128)S(1)} fusion(f32[8,32]{1,0:T(8,128)S(1)} %fusion.33, f32[9,2,24,32]{3,2,1,0:T(8,128)S(1)} %maximum_maximum_fusion, s32[32]{0:T(128)S(1)} %get-tuple-element.67), kind=kOutput, calls=%fused_computation.1 | convolution fusion | flops 85049344 | bytes 1825920 | tf_op jit(solution)/shard_map/dot_general | solution.py:355
  35.5 6.7 %collective-permute-done.3.hyu_ref = f32[24,18,128]{2,1,0:T(8,128)S(1)} collective-permute-done((f32[24,18,128]{2,1,0:T(8,128)S(1)}, f32[24,18,128]{2,1,0:T(8,128)S(1)}, u32[]{:S(2)}, u32[]{:S(2)}) %collective-permute-start.3) | collective-permute-done | bytes 221216 | tf_op jit(solution)/shard_map/ppermute | solution.py:31
  42.2 0.7 %copy-done.5 = f32[24,18,128]{2,1,0:T(8,128)} copy-done((f32[24,18,128]{2,1,0:T(8,128)}, f32[24,18,128]{2,1,0:T(8,128)S(1)}, u32[]{:S(2)}) %copy-start.5) | copy-done | bytes 221208
  43.0 0.7 %copy-done.4 = f32[24,20,128]{2,1,0:T(8,128)} copy-done((f32[24,20,128]{2,1,0:T(8,128)}, f32[24,20,128]{2,1,0:T(8,128)S(1)}, u32[]{:S(2)}) %copy-start.4) | copy-done | bytes 245784
  43.7 7.1 %shard_map.203 = (f32[2,24,8,128]{3,2,1,0:T(8,128)}, f32[4,2,24,8,128]{4,3,2,1,0:T(8,128)}, f32[4,2,24,8,128]{4,3,2,1,0:T(8,128)}) custom-call(f32[24,8,128]{2,1,0:T(8,128)} %pn_ref, f32[24,8,128]{2,1,0:T(8,128)} %sn_ref, f32[24,8,128]{2,1,0:T(8,128)} %so_ref.1, f32[24,8,128]{2,1,0:T(8,128)} %pore_ref.1, f32[24,8,128]{2,1,0:T(8,128)} %tx_ref.3, ...), custom_call_target="tpu_custom_call" | custom-call | flops 29491200 | bytes 9043968 | tf_op jit(solution)/shard_map/pallas_call | solution.py:372
  50.8 1.6 %fusion.12 = f32[2,24,8,128]{3,2,1,0:T(8,128)} fusion(f32[2,24,8,128]{3,2,1,0:T(8,128)} %get-tuple-element.30, f32[9,2,24,8,128]{4,3,2,1,0:T(8,128)S(1)} %fusion), kind=kLoop, calls=%fused_computation.22 | loop fusion | flops 49152 | bytes 589824 | tf_op jit(solution)/shard_map/add | solution.py:421
  52.4 2.7 %slice_add_fusion = (f32[4,2,24,8,128]{4,3,2,1,0:T(8,128)}, f32[4,2,24,8,128]{4,3,2,1,0:T(8,128)}) fusion(f32[4,2,24,8,128]{4,3,2,1,0:T(8,128)} %get-tuple-element.32, f32[9,2,24,8,128]{4,3,2,1,0:T(8,128)S(1)} %fusion, f32[4,2,24,8,128]{4,3,2,1,0:T(8,128)} %get-tuple-element.31), kind=kLoop, calls=%fused_computation.14 | loop fusion | flops 393216 | bytes 4718592 | tf_op jit(solution)/shard_map/add | solution.py:423
  (64 shorter events, 0.9 us)
Async XLA Ops:
  0.6 7.8 %copy-start.1 = (f32[4,2,24,8,128]{4,3,2,1,0:T(8,128)S(1)}, f32[4,2,24,8,128]{4,3,2,1,0:T(8,128)}, u32[]{:S(2)}) copy-start(f32[4,2,24,8,128]{4,3,2,1,0:T(8,128)} %wn_ref) | copy-start | bytes 2359300
  0.6 8.5 %copy-start = (f32[4,2,24,8,128]{4,3,2,1,0:T(8,128)S(1)}, f32[4,2,24,8,128]{4,3,2,1,0:T(8,128)}, u32[]{:S(2)}) copy-start(f32[4,2,24,8,128]{4,3,2,1,0:T(8,128)} %dn_ref) | copy-start | bytes 2359300
  0.7 7.5 %copy-start.3 = (f32[24,8,128]{2,1,0:T(8,128)S(1)}, f32[24,8,128]{2,1,0:T(8,128)}, u32[]{:S(2)}) copy-start(f32[24,8,128]{2,1,0:T(8,128)} %sn_ref) | copy-start | bytes 294916
  0.7 7.2 %copy-start.2 = (f32[24,8,128]{2,1,0:T(8,128)S(1)}, f32[24,8,128]{2,1,0:T(8,128)}, u32[]{:S(2)}) copy-start(f32[24,8,128]{2,1,0:T(8,128)} %pn_ref) | copy-start | bytes 294916
  2.9 7.0 %copy-start.8 = (f32[2048]{0:T(1024)S(1)}, f32[2048]{0:T(1024)}, u32[]{:S(2)}) copy-start(f32[2048]{0:T(1024)} %param.37) | copy-start | bytes 24580
  2.9 7.0 %copy-start.9 = (f32[2048]{0:T(1024)S(1)}, f32[2048]{0:T(1024)}, u32[]{:S(2)}) copy-start(f32[2048]{0:T(1024)} %param.36) | copy-start | bytes 24580
  7.9 3.1 %copy-start.11 = (s32[32]{0:T(128)S(1)}, s32[32]{0:T(128)}, u32[]{:S(2)}) copy-start(s32[32]{0:T(128)} %param.33) | copy-start | bytes 388
  7.9 3.1 %copy-start.16 = (s32[32]{0:T(128)S(1)}, s32[32]{0:T(128)}, u32[]{:S(2)}) copy-start(s32[32]{0:T(128)} %param.34) | copy-start | bytes 388
  7.9 3.1 %copy-start.10 = (f32[32]{0:T(128)S(1)}, f32[32]{0:T(128)}, u32[]{:S(2)}) copy-start(f32[32]{0:T(128)} %param.35) | copy-start | bytes 388
  9.2 13.6 %copy-start.14 = (f32[24,8,20]{2,1,0:T(8,128)S(1)}, f32[24,8,20]{2,1,0:T(8,128)}, u32[]{:S(2)}) copy-start(f32[24,8,20]{2,1,0:T(8,128)} %get-tuple-element.26) | copy-start | bytes 46084
  9.2 16.7 %copy-start.15 = (f32[24,8,18]{2,1,0:T(8,128)S(1)}, f32[24,8,18]{2,1,0:T(8,128)}, u32[]{:S(2)}) copy-start(f32[24,8,18]{2,1,0:T(8,128)} %get-tuple-element.27) | copy-start | bytes 41476
  9.2 18.9 %copy-start.12 = (f32[24,20,128]{2,1,0:T(8,128)S(1)}, f32[24,20,128]{2,1,0:T(8,128)}, u32[]{:S(2)}) copy-start(f32[24,20,128]{2,1,0:T(8,128)} %get-tuple-element.28) | copy-start | bytes 737284
  9.2 22.9 %copy-start.13 = (f32[24,18,128]{2,1,0:T(8,128)S(1)}, f32[24,18,128]{2,1,0:T(8,128)}, u32[]{:S(2)}) copy-start(f32[24,18,128]{2,1,0:T(8,128)} %get-tuple-element.29) | copy-start | bytes 663556
  12.2 21.8 %all-to-all-start = ((f32[128,1,352]{2,1,0:T(1,128)}), f32[128,1,352]{2,1,0:T(1,128)S(1)}, u32[]{:S(2)}, u32[]{:S(2)}) async-start(f32[128,1,352]{2,1,0:T(1,128)} %broadcast_in_dim.43), calls=%async_computation | async-start | bytes 393216 | tf_op jit(solution)/shard_map/all_to_all | solution.py:23
  22.7 12.8 %collective-permute-start = (f32[24,8,20]{2,1,0:T(8,128)S(1)}, f32[24,8,20]{2,1,0:T(8,128)S(1)}, u32[]{:S(2)}, u32[]{:S(2)}) collective-permute-start(f32[24,8,20]{2,1,0:T(8,128)S(1)} %copy-done.14), channel_id=1, source_target_pairs={{0,32},{32,64},{64,96},{1,33},{33,65},{65,97},{2,34},{34,66},{66,9... | collective-permute-start | bytes 46088 | tf_op jit(solution)/shard_map/ppermute | solution.py:31
  25.9 9.6 %collective-permute-start.1 = (f32[24,8,18]{2,1,0:T(8,128)S(1)}, f32[24,8,18]{2,1,0:T(8,128)S(1)}, u32[]{:S(2)}, u32[]{:S(2)}) collective-permute-start(f32[24,8,18]{2,1,0:T(8,128)S(1)} %copy-done.15), channel_id=1, source_target_pairs={{32,0},{64,32},{96,64},{33,1},{65,33},{97,65},{34,2},{66,34},{98,6... | collective-permute-start | bytes 41480 | tf_op jit(solution)/shard_map/ppermute | solution.py:31
  28.1 14.2 %collective-permute-start.2 = (f32[24,20,128]{2,1,0:T(8,128)S(1)}, f32[24,20,128]{2,1,0:T(8,128)S(1)}, u32[]{:S(2)}, u32[]{:S(2)}) collective-permute-start(f32[24,20,128]{2,1,0:T(8,128)S(1)} %copy-done.12), channel_id=1, source_target_pairs={{0,1},{1,2},{2,3},{3,4},{4,5},{5,6},{6,7},{7,8},{8,9},{9,10},{10,1... | collective-permute-start | bytes 737288 | tf_op jit(solution)/shard_map/ppermute | solution.py:31
  32.1 10.2 %collective-permute-start.3 = (f32[24,18,128]{2,1,0:T(8,128)S(1)}, f32[24,18,128]{2,1,0:T(8,128)S(1)}, u32[]{:S(2)}, u32[]{:S(2)}) collective-permute-start(f32[24,18,128]{2,1,0:T(8,128)S(1)} %copy-done.13), channel_id=1, source_target_pairs={{1,0},{2,1},{3,2},{4,3},{5,4},{6,5},{7,6},{8,7},{9,8},{10,9},{11,1... | collective-permute-start | bytes 663560 | tf_op jit(solution)/shard_map/ppermute | solution.py:31
  35.5 6.7 %copy-start.7 = (f32[24,8,18]{2,1,0:T(8,128)}, f32[24,8,18]{2,1,0:T(8,128)S(1)}, u32[]{:S(2)}) copy-start(f32[24,8,18]{2,1,0:T(8,128)S(1)} %collective-permute-done.1.hxr_ref) | copy-start | bytes 41476
  35.5 6.7 %copy-start.6 = (f32[24,8,20]{2,1,0:T(8,128)}, f32[24,8,20]{2,1,0:T(8,128)S(1)}, u32[]{:S(2)}) copy-start(f32[24,8,20]{2,1,0:T(8,128)S(1)} %collective-permute-done.hxl_ref) | copy-start | bytes 46084
  42.2 0.7 %copy-start.5 = (f32[24,18,128]{2,1,0:T(8,128)}, f32[24,18,128]{2,1,0:T(8,128)S(1)}, u32[]{:S(2)}) copy-start(f32[24,18,128]{2,1,0:T(8,128)S(1)} %collective-permute-done.3.hyu_ref) | copy-start | bytes 663556
  43.0 0.7 %copy-start.4 = (f32[24,20,128]{2,1,0:T(8,128)}, f32[24,20,128]{2,1,0:T(8,128)S(1)}, u32[]{:S(2)}) copy-start(f32[24,20,128]{2,1,0:T(8,128)S(1)} %collective-permute-done.2.hyd_ref) | copy-start | bytes 737284
